TPU v7x, 1024 devices: a whole 4x4x32 slice. The times are simulated.
1024 devices in a mesh: lev: 16 (over y, x), wave: 64 (over z, core).
Axes of the slice: x: 4, y: 4, z: 32, core: 2. Of those that a mesh axis runs over, the one named last changes fastest.
Arguments:
- spectral: bfloat16 [128, 512, 3, 2, 512], P('lev', 'wave'), may hold values from -6 to 6
- modes_in: bfloat16 [128, 128], replicated, may hold values from -0.5 to 0.5
- modes_out: bfloat16 [128, 128], replicated, may hold values from -0.5 to 0.5
- mode_depth: float32 [128], replicated, may hold values from 0.1 to 10
- legendre: bfloat16 [512, 512, 256], P('wave'), may hold values from -0.25 to 0.25
- wave_map: int32 [512], replicated, may hold values from 0 to 511, as said below
- row_points: int32 [256], P('wave'), may hold values from 320 to 1280, as said below
Outputs:
- advected: float32 [3, 128, 256, 1280], P(None, 'lev', 'wave')
Inputs may be any that keep to these rules, and one draw needn't show every extreme that they name: `wave_map`: a permutation of 0 to 511; the entries at slots 2 k and 2 k + 1 add up to 511. `row_points`: some row has all 1280 points.
All inputs are finite; a program needn't handle non-finite values.
Results may differ from a plain program's by a relative error of at most 0.0059.
Values may be sent and summed in bfloat16 or wider, within the bound.
No kernel may reach another device: no remote copies, remote signals or barrier semaphores. Data moves between devices by JAX's collectives and lax.ppermute only.
A program may use at most 32 MiB of HBM per device.

v0:
```python
import math

import jax
import jax.numpy as jnp
from jax import lax
from jax.sharding import PartitionSpec as P

LON = 1280


time_step = 0.8


def with_halo(value, sides, width):
    for axis, dim in sides:
        size, length = (lax.axis_size(axis), value.shape[dim])
        up = [(i, (i + 1) % size) for i in range(size - 1)]
        down = [(j, i) for i, j in up]
        last = lax.slice_in_dim(value, length - width, length, axis=dim)
        leading = lax.slice_in_dim(value, 0, width, axis=dim)
        before = lax.ppermute(last, axis, up)
        after = lax.ppermute(leading, axis, down)
        value = jnp.concatenate([before, value, after], axis=dim)
    return value


def damping(mode_depth, degree_of, degree_total):
    ratio = degree_of * (degree_of + 1.0) / float(degree_total * degree_total)
    return 1.0 / (1.0 + mode_depth[:, None] * ratio[None, :])


def trig_table(wave_map, lon_count):
    column = jnp.arange(lon_count, dtype=jnp.int32)
    product = wave_map[:, None] * column[None, :] % lon_count
    angles = product.astype(jnp.float32) * (2.0 * math.pi / lon_count)
    return jnp.stack([jnp.cos(angles), -jnp.sin(angles)], axis=1).astype(jnp.bfloat16)


def tendency(fields_ext):
    center = fields_ext[..., 1:-1, :]
    ahead_lon = jnp.roll(center, -1, axis=-1)
    behind_lon = jnp.roll(center, 1, axis=-1)
    ahead_lat = fields_ext[..., 2:, :]
    behind_lat = fields_ext[..., :-2, :]
    return center[0] * (ahead_lon - behind_lon) * 0.5 + center[1] * (ahead_lat - behind_lat) * 0.5


def column_solve(columns, modes_in, modes_out, mode_depth, degree_count):
    column_count = columns.shape[1]
    column_ids = lax.axis_index("lev") * column_count + jnp.arange(column_count, dtype=jnp.int32)
    degree_of = (column_ids % degree_count).astype(jnp.float32)
    modal_part = jnp.dot(modes_in, columns, preferred_element_type=jnp.float32)
    scaled = (modal_part * damping(mode_depth, degree_of, degree_count)).astype(jnp.bfloat16)
    return jnp.dot(modes_out, scaled, preferred_element_type=jnp.float32).astype(jnp.bfloat16)


def per_device(spectral, modes_in, modes_out, mode_depth, legendre, wave_map, row_points):
    lev_rows = spectral.shape[0]
    wave_slots = spectral.shape[1]
    field_count = spectral.shape[2]
    degree_count = spectral.shape[4]
    levels = modes_in.shape[0]
    shard_count = lax.axis_size("wave")
    first_slot = lax.axis_index("wave") * wave_slots
    local_waves = lax.dynamic_slice_in_dim(wave_map, first_slot, wave_slots)
    degrees = jnp.arange(degree_count, dtype=jnp.int32)
    keep_mask = degrees[None, :] >= local_waves[:, None]
    masked = jnp.where(keep_mask[None, :, None, None, :], spectral, jnp.zeros_like(spectral))
    flattened = masked.reshape(lev_rows, -1)
    trig_rows = trig_table(wave_map, LON).reshape(shard_count, wave_slots, 2, LON)
    norm_factor = 1.0 / math.sqrt(wave_map.shape[0])
    columns = lax.all_to_all(flattened, "lev", split_axis=1, concat_axis=0, tiled=True)
    solved_cols = column_solve(columns, modes_in, modes_out, mode_depth, degree_count)
    group_count = solved_cols.shape[1] // degree_count
    group_ids = lax.axis_index("lev") * group_count + jnp.arange(group_count, dtype=jnp.int32)
    slot_ids = group_ids // (field_count * 2)
    picked = jnp.take(legendre, slot_ids, axis=0)
    solved_groups = solved_cols.reshape(levels, group_count, degree_count)
    band_cols = jnp.einsum(
        "lgn,gnt->tgl", solved_groups, picked, preferred_element_type=jnp.float32
    ).astype(jnp.bfloat16)
    arrived = lax.all_to_all(
        lax.all_to_all(band_cols, "lev", split_axis=2, concat_axis=1, tiled=True),
        "wave",
        split_axis=0,
        concat_axis=2,
        tiled=True,
    )
    lat_rows = arrived.shape[0]
    split_bands = arrived.reshape(lat_rows, wave_slots, field_count, 2, shard_count, lev_rows)
    grid_field = (
        jnp.einsum("tsfcwl,wscx->fltx", split_bands, trig_rows, preferred_element_type=jnp.float32)
        * norm_factor
    )
    wide_rows = with_halo(grid_field, (("wave", 2),), 2)
    section_wide = wide_rows[:, :, 1:-1, :] - time_step * tendency(wide_rows)
    second = 0.5 * (grid_field + section_wide[:, :, 1:-1, :] - time_step * tendency(section_wide))
    points = jnp.arange(LON, dtype=jnp.int32)[None, :] < row_points[:, None]
    return jnp.where(points[None, None, :, :], second, jnp.zeros_like(second))


def solution(mesh):
    in_specs = (
        P("lev", "wave", None, None, None),
        P(),
        P(),
        P(),
        P("wave", None, None),
        P(),
        P("wave"),
    )
    out_specs = P(None, "lev", "wave", None)
    return jax.shard_map(
        per_device, mesh=mesh, in_specs=in_specs, out_specs=out_specs, check_vma=False
    )
```

profile of v0, /device:TPU:1, one launch (start us, length us, event | category | flops | bytes accessed | tf_op | source)
XLA Modules:
  0.0 121.2 jit_solution(5474963246780085542)
XLA Ops:
  0.0 0.9 dynamic_slice.3
  1.0 1.3 %broadcast_select_fusion = bf16[8,8,3,2,512]{4,3,2,1,0:T(2,128)(2,1)S(1)} fusion(bf16[8,8,3,2,512]{4,3,2,1,0:T(2,128)(2,1)} %param.7, pred[8,512]{1,0:T(8,128)(4,1)S(1)} %iota_compare_fusion.1), kind=kLoop, calls=%fused_computation.29 | loop fusion | flops 196608 | bytes 790528 | tf_op jit(solution)/shard_map/jit(_where)/select_n | solution.py:68
  2.6 1.0 copy.42
  3.6 7.6 %all-to-all-start = ((bf16[8,16,1536]{2,0,1:T(8,128)(2,1)}), bf16[8,16,1536]{2,0,1:T(8,128)(2,1)S(1)}, u32[]{:S(2)}, u32[]{:S(2)}) async-start(bf16[8,16,1536]{2,0,1:T(8,128)(2,1)} %copy.42), calls=%async_computation | async-start | bytes 786432 | tf_op jit(solution)/shard_map/all_to_all | solution.py:72
  11.2 0.6 gather_fusion
  11.8 7.5 %all-to-all-done = bf16[8,16,1536]{2,0,1:T(8,128)(2,1)S(1)} async-done(((bf16[8,16,1536]{2,0,1:T(8,128)(2,1)}), bf16[8,16,1536]{2,0,1:T(8,128)(2,1)S(1)}, u32[]{:S(2)}, u32[]{:S(2)}) %all-to-all-start) | async-done | bytes 393248 | tf_op jit(solution)/shard_map/all_to_all | solution.py:72
  19.4 1.3 %convolution_convert_fusion = bf16[1536,128]{1,0:T(8,128)(2,1)} fusion(bf16[128,128]{1,0:T(8,128)(2,1)S(1)} %copy-done.3, bf16[128,128]{1,0:T(8,128)(2,1)S(1)} %copy-done.4, bf16[8,16,1536]{2,0,1:T(8,128)(2,1)S(1)} %all-to-all-done, f32[1536]{0:T(1024)S(1)} %fusion.43, f32[128]{0:T(128)S(1)} %copy-done.5), kind=kOutput, calls=%fused_computation.20 | convolution fusion | flops 101842944 | bytes 858624 | tf_op jit(solution)/shard_map/dot_general | solution.py:54
  20.7 1.5 %fusion.13 = bf16[256,3,128]{2,0,1:T(8,128)(2,1)S(1)} fusion(bf16[128,3,512]{0,2,1:T(8,128)(2,1)} %bitcast.71, bf16[3,512,256]{2,1,0:T(8,128)(2,1)S(1)} %gather_fusion, pred[3]{0:T(512)(128)(4,1)S(1)} %compare_and_fusion), kind=kOutput, calls=%fused_computation.22 | convolution fusion | flops 101154816 | bytes 1376259 | tf_op jit(solution)/shard_map/lgn,gnt->tgl/dot_general | solution.py:79
  22.4 10.2 %all_to_all.52 = bf16[256,3,128]{0,1,2:T(4,128)(2,1)S(1)} all-to-all(bf16[256,3,128]{0,1,2:T(4,128)(2,1)S(1)} %copy.45), channel_id=1, replica_groups=mesh['lev'=16,'wave'=64] {'lev'}, dimensions={2} | all-to-all | bytes 393216 | tf_op jit(solution)/shard_map/all_to_all | solution.py:83
  32.6 0.4 copy.48
  33.0 1.4 %reshape.199 = bf16[64,2,768]{2,1,0:T(2,128)(2,1)} reshape(bf16[256,8,48]{2,1,0:T(8,128)(2,1)S(1)} %bitcast.67) | data formatting | bytes 393216
  34.4 33.1 %all-to-all-start.2 = ((bf16[64,2,768]{2,1,0:T(2,128)(2,1)}), bf16[64,2,768]{2,1,0:T(2,128)(2,1)S(1)}, u32[]{:S(2)}, u32[]{:S(2)}) async-start(bf16[64,2,768]{2,1,0:T(2,128)(2,1)} %reshape.199), calls=%async_computation.2 | async-start | bytes 393216 | tf_op jit(solution)/shard_map/all_to_all | solution.py:82
  67.7 13.0 %cosine_convert_fusion = (bf16[64,8,1,1280]{3,0,1,2:T(8,128)(2,1)}, bf16[64,8,1,1280]{3,0,1,2:T(8,128)(2,1)}) fusion(s32[64,8]{0,1:T(8,128)S(1)} %copy.41), kind=kLoop, calls=%fused_computation.9 | loop fusion | flops 7864320 | bytes 2623488 | tf_op jit(solution)/shard_map/convert
  80.7 23.3 %all-to-all-done.2 = bf16[64,2,768]{2,1,0:T(2,128)(2,1)S(1)} async-done(((bf16[64,2,768]{2,1,0:T(2,128)(2,1)}), bf16[64,2,768]{2,1,0:T(2,128)(2,1)S(1)}, u32[]{:S(2)}, u32[]{:S(2)}) %all-to-all-start.2) | async-done | bytes 196640 | tf_op jit(solution)/shard_map/all_to_all | solution.py:82
  104.0 0.5 reshape.200
  104.5 0.7 copy.49
  105.2 2.3 %fusion.12 = f32[3,8,4,1280]{3,1,0,2:T(8,128)S(1)} fusion(bf16[64,8,1,1280]{3,0,1,2:T(8,128)(2,1)} %get-tuple-element.18, bf16[64,8,1,1280]{3,0,1,2:T(8,128)(2,1)} %get-tuple-element.17, bf16[4,8,3,2,64,8]{4,5,3,2,1,0:T(8,128)(2,1)S(1)} %bitcast.70), kind=kOutput, calls=%fused_computation.19 | convolution fusion | flops 257024000 | bytes 3309568 | tf_op jit(solution)/shard_map/tsfcwl,wscx->fltx/dot_general | solution.py:92
  107.6 3.7 %collective-permute-start = (f32[3,8,2,1280]{3,1,0,2:T(8,128)S(1)}, f32[3,8,2,1280]{3,1,0,2:T(8,128)S(1)}, u32[]{:S(2)}, u32[]{:S(2)}) collective-permute-start(f32[3,8,2,1280]{3,1,0,2:T(8,128)S(1)} %get-tuple-element.15), channel_id=1, source_target_pairs={{0,1},{1,2},{2,3},{3,4},{4,5},{5,6},{6,7},{7,8},{8,9},{9,10},{10,1... | collective-permute-start | bytes 737288 | tf_op jit(solution)/shard_map/ppermute | solution.py:21
  111.3 1.9 %collective-permute-start.1 = (f32[3,8,2,1280]{3,1,0,2:T(8,128)S(1)}, f32[3,8,2,1280]{3,1,0,2:T(8,128)S(1)}, u32[]{:S(2)}, u32[]{:S(2)}) collective-permute-start(f32[3,8,2,1280]{3,1,0,2:T(8,128)S(1)} %get-tuple-element.16), channel_id=1, source_target_pairs={{1,0},{2,1},{3,2},{4,3},{5,4},{6,5},{7,6},{8,7},{9,8},{10,9},{11,1... | collective-permute-start | bytes 737288 | tf_op jit(solution)/shard_map/ppermute | solution.py:22
  113.3 1.1 collective-permute-done
  114.4 4.4 %collective-permute-done.1 = f32[3,8,2,1280]{3,1,0,2:T(8,128)S(1)} collective-permute-done((f32[3,8,2,1280]{3,1,0,2:T(8,128)S(1)}, f32[3,8,2,1280]{3,1,0,2:T(8,128)S(1)}, u32[]{:S(2)}, u32[]{:S(2)}) %collective-permute-start.1) | collective-permute-done | bytes 245792 | tf_op jit(solution)/shard_map/ppermute | solution.py:22
  119.2 0.4 fusion.24
  119.9 0.3 fusion.32
  120.2 1.0 copy.51
  (31 shorter events, 1.6 us)
Async XLA Ops:
  0.0 11.2 %copy-start = (bf16[8,512,256]{2,1,0:T(8,128)(2,1)S(1)}, bf16[8,512,256]{2,1,0:T(8,128)(2,1)}, u32[]{:S(2)}) copy-start(bf16[8,512,256]{2,1,0:T(8,128)(2,1)} %param.11) | copy-start | bytes 6291460
  2.3 17.1 %copy-start.3 = (bf16[128,128]{1,0:T(8,128)(2,1)S(1)}, bf16[128,128]{1,0:T(8,128)(2,1)}, u32[]{:S(2)}) copy-start(bf16[128,128]{1,0:T(8,128)(2,1)} %param.9) | copy-start | bytes 98308
  2.3 17.1 %copy-start.4 = (bf16[128,128]{1,0:T(8,128)(2,1)S(1)}, bf16[128,128]{1,0:T(8,128)(2,1)}, u32[]{:S(2)}) copy-start(bf16[128,128]{1,0:T(8,128)(2,1)} %param.8) | copy-start | bytes 98308
  2.3 17.1 %copy-start.5 = (f32[128]{0:T(128)S(1)}, f32[128]{0:T(128)}, u32[]{:S(2)}) copy-start(f32[128]{0:T(128)} %param.10) | copy-start | bytes 1540
  3.6 15.8 %all-to-all-start = ((bf16[8,16,1536]{2,0,1:T(8,128)(2,1)}), bf16[8,16,1536]{2,0,1:T(8,128)(2,1)S(1)}, u32[]{:S(2)}, u32[]{:S(2)}) async-start(bf16[8,16,1536]{2,0,1:T(8,128)(2,1)} %copy.42), calls=%async_computation | async-start | bytes 786432 | tf_op jit(solution)/shard_map/all_to_all | solution.py:72
  22.2 45.3 %copy-start.1 = (s32[512]{0:T(512)S(1)}, s32[512]{0:T(512)}, u32[]{:S(2)}) copy-start(s32[512]{0:T(512)} %param.12) | copy-start | bytes 6148
  34.4 69.6 %all-to-all-start.2 = ((bf16[64,2,768]{2,1,0:T(2,128)(2,1)}), bf16[64,2,768]{2,1,0:T(2,128)(2,1)S(1)}, u32[]{:S(2)}, u32[]{:S(2)}) async-start(bf16[64,2,768]{2,1,0:T(2,128)(2,1)} %reshape.199), calls=%async_computation.2 | async-start | bytes 393216 | tf_op jit(solution)/shard_map/all_to_all | solution.py:82
  105.2 8.0 %copy-start.2 = (s32[4]{0:T(128)S(1)}, s32[4]{0:T(128)}, u32[]{:S(2)}) copy-start(s32[4]{0:T(128)} %param.13) | copy-start | bytes 52
  107.6 6.8 %collective-permute-start = (f32[3,8,2,1280]{3,1,0,2:T(8,128)S(1)}, f32[3,8,2,1280]{3,1,0,2:T(8,128)S(1)}, u32[]{:S(2)}, u32[]{:S(2)}) collective-permute-start(f32[3,8,2,1280]{3,1,0,2:T(8,128)S(1)} %get-tuple-element.15), channel_id=1, source_target_pairs={{0,1},{1,2},{2,3},{3,4},{4,5},{5,6},{6,7},{7,8},{8,9},{9,10},{10,1... | collective-permute-start | bytes 737288 | tf_op jit(solution)/shard_map/ppermute | solution.py:21
  111.3 7.5 %collective-permute-start.1 = (f32[3,8,2,1280]{3,1,0,2:T(8,128)S(1)}, f32[3,8,2,1280]{3,1,0,2:T(8,128)S(1)}, u32[]{:S(2)}, u32[]{:S(2)}) collective-permute-start(f32[3,8,2,1280]{3,1,0,2:T(8,128)S(1)} %get-tuple-element.16), channel_id=1, source_target_pairs={{1,0},{2,1},{3,2},{4,3},{5,4},{6,5},{7,6},{8,7},{9,8},{10,9},{11,1... | collective-permute-start | bytes 737288 | tf_op jit(solution)/shard_map/ppermute | solution.py:22
where the time goes:
time: 122 us; the launch traced here: 121 us
  starting transfers between devices  46.3 us (38%)
  waiting for transfers between devices  36.3 us (30%)
  other arithmetic  15.3 us (13%)
  blocking collectives  10.2 us (8%)
  local copies, waits for them, and re-layouts  7.67 us (6%)
  matrix products  5.09 us (4%)
    all_to_all x1, starting transfers between devices, per_device(): lax.all_to_all(lax.all_to_all(band_cols, 'lev', split_axis=2, concat_axis...  33.1 us
    all_to_all x1, waiting for transfers between devices, per_device(): lax.all_to_all(lax.all_to_all(band_cols, 'lev', split_axis=2, concat_axis...  23.3 us
    another operation x1, other arithmetic  13 us
    all_to_all x1, blocking collectives, per_device(): lax.all_to_all(band_cols, 'lev', split_axis=2, concat_axis=1, tiled=True)  10.2 us
    all_to_all x1, starting transfers between devices, per_device(): lax.all_to_all(flattened, 'lev', split_axis=1, concat_axis=0, tiled=True)  7.57 us
    all_to_all x1, waiting for transfers between devices, per_device(): lax.all_to_all(flattened, 'lev', split_axis=1, concat_axis=0, tiled=True)  7.54 us
    ppermute x1, waiting for transfers between devices, with_halo(): after = lax.ppermute(leading, axis, down)  4.4 us
    ppermute x1, starting transfers between devices, with_halo(): before = lax.ppermute(last, axis, up)  3.72 us
  transfers between devices with their start and end apart: 4, of which 4 were waited for; matrix products, arithmetic and copies ran while one was open for 11% of the time, Pallas kernels for 0%

commit v1 on v0

--- a/solution.py
+++ b/solution.py
@@ -29,11 +29,18 @@
     return 1.0 / (1.0 + mode_depth[:, None] * ratio[None, :])
 
 
-def trig_table(wave_map, lon_count):
-    column = jnp.arange(lon_count, dtype=jnp.int32)
-    product = wave_map[:, None] * column[None, :] % lon_count
-    angles = product.astype(jnp.float32) * (2.0 * math.pi / lon_count)
-    return jnp.stack([jnp.cos(angles), -jnp.sin(angles)], axis=1).astype(jnp.bfloat16)
+def trig_table(wave_map, lon_count, block=32):
+    waves = wave_map[:, None]
+    coarse = waves * (jnp.arange(lon_count // block, dtype=jnp.int32)[None, :] * block) % lon_count
+    fine = waves * jnp.arange(block, dtype=jnp.int32)[None, :] % lon_count
+    step = 2.0 * math.pi / lon_count
+    coarse_angle = coarse.astype(jnp.float32) * step
+    fine_angle = fine.astype(jnp.float32) * step
+    cos_c, sin_c = jnp.cos(coarse_angle)[:, :, None], jnp.sin(coarse_angle)[:, :, None]
+    cos_f, sin_f = jnp.cos(fine_angle)[:, None, :], jnp.sin(fine_angle)[:, None, :]
+    cos_all = (cos_c * cos_f - sin_c * sin_f).reshape(wave_map.shape[0], lon_count)
+    sin_all = (sin_c * cos_f + cos_c * sin_f).reshape(wave_map.shape[0], lon_count)
+    return jnp.stack([cos_all, -sin_all], axis=1).astype(jnp.bfloat16)
 
 
 def tendency(fields_ext):
@@ -79,17 +86,16 @@
     band_cols = jnp.einsum(
         "lgn,gnt->tgl", solved_groups, picked, preferred_element_type=jnp.float32
     ).astype(jnp.bfloat16)
-    arrived = lax.all_to_all(
-        lax.all_to_all(band_cols, "lev", split_axis=2, concat_axis=1, tiled=True),
-        "wave",
-        split_axis=0,
-        concat_axis=2,
-        tiled=True,
-    )
-    lat_rows = arrived.shape[0]
-    split_bands = arrived.reshape(lat_rows, wave_slots, field_count, 2, shard_count, lev_rows)
+    lev_count = lax.axis_size("lev")
+    lat_rows = band_cols.shape[0] // shard_count
+    outgoing = band_cols.reshape(shard_count, lat_rows, group_count, lev_count, lev_rows)
+    outgoing = outgoing.transpose(3, 0, 1, 2, 4).reshape(lev_count * shard_count, -1)
+    incoming = lax.all_to_all(outgoing, ("lev", "wave"), 0, 0, tiled=True)
+    incoming = incoming.reshape(lev_count, shard_count, lat_rows, group_count, lev_rows)
+    arrived = incoming.transpose(2, 1, 0, 3, 4).reshape(lat_rows, -1, lev_rows)
+    split_bands = arrived.reshape(lat_rows, shard_count, wave_slots, field_count, 2, lev_rows)
     grid_field = (
-        jnp.einsum("tsfcwl,wscx->fltx", split_bands, trig_rows, preferred_element_type=jnp.float32)
+        jnp.einsum("twsfcl,wscx->fltx", split_bands, trig_rows, preferred_element_type=jnp.float32)
         * norm_factor
     )
     wide_rows = with_halo(grid_field, (("wave", 2),), 2)

time: 122 us -> 152 us (1.25)
  local copies, waits for them, and re-layouts: 7.67 us -> 31.4 us
  blocking collectives: 10.2 us -> 0 us
  starting transfers between devices: 46.3 us -> 56.3 us
  waiting for transfers between devices: 36.3 us -> 44.9 us
  other arithmetic: 15.3 us -> 12.2 us
    all_to_all x1, waiting for transfers between devices: 23.3 us -> 34.3 us  [per_device(): incoming = lax.all_to_all(outgoing, ('lev', 'wave'), 0, 0, tiled=True)]
    all_to_all x1 -> x0, blocking collectives: 10.2 us -> none  [per_device(): lax.all_to_all(band_cols, 'lev', split_axis=2, concat_axis=1, tiled=True)]
    all_to_all x1, starting transfers between devices: 33.1 us -> 43.2 us  [per_device(): incoming = lax.all_to_all(outgoing, ('lev', 'wave'), 0, 0, tiled=True)]
    neg x0 -> x2, local copies, waits for them, and re-layouts: none -> 7.34 us  [trig_table(): return jnp.stack([cos_all, -sin_all], axis=1).astype(jnp.bfloat16)]
    sub x0 -> x2, local copies, waits for them, and re-layouts: none -> 7.31 us  [trig_table(): cos_c * cos_f - sin_c * sin_f]
    another operation x1, other arithmetic: 13 us -> 7.66 us
    transpose x0 -> x2, local copies, waits for them, and re-layouts: none -> 5.08 us  [the longest x1 4.98 us: per_device(): outgoing.transpose(3, 0, 1, 2, 4).reshape(lev_count * shard_count, -1)]
    reshape x0 -> x2, local copies, waits for them, and re-layouts: none -> 4.81 us  [the longest x1 4.54 us: per_device(): band_cols.reshape(shard_count, lat_rows, group_count, lev_count, lev_rows)]
  transfers between devices with their start and end apart: 4 -> 4, of which waited for: 4 -> 4; matrix products, arithmetic and copies ran while one was open for 11% -> 17% of each run, Pallas kernels for 0% -> 0%
where the time goes in v1:
time: 152 us; the launch traced here: 151 us
  starting transfers between devices  56.3 us (37%)
  waiting for transfers between devices  44.9 us (30%)
  local copies, waits for them, and re-layouts  31.4 us (21%)
  other arithmetic  12.2 us (8%)
  matrix products  5.88 us (4%)
    all_to_all x1, starting transfers between devices, per_device(): incoming = lax.all_to_all(outgoing, ('lev', 'wave'), 0, 0, tiled=True)  43.2 us
    all_to_all x1, waiting for transfers between devices, per_device(): incoming = lax.all_to_all(outgoing, ('lev', 'wave'), 0, 0, tiled=True)  34.3 us
    another operation x1, other arithmetic  7.66 us
    all_to_all x1, starting transfers between devices, per_device(): lax.all_to_all(flattened, 'lev', split_axis=1, concat_axis=0, tiled=True)  7.57 us
    all_to_all x1, waiting for transfers between devices, per_device(): lax.all_to_all(flattened, 'lev', split_axis=1, concat_axis=0, tiled=True)  7.54 us
    neg x2, local copies, waits for them, and re-layouts, trig_table(): return jnp.stack([cos_all, -sin_all], axis=1).astype(jnp.bfloat16)  7.34 us
    sub x2, local copies, waits for them, and re-layouts, trig_table(): cos_c * cos_f - sin_c * sin_f  7.31 us
    transpose x1, local copies, waits for them, and re-layouts, per_device(): outgoing.transpose(3, 0, 1, 2, 4).reshape(lev_count * shard_count, -1)  4.98 us
  transfers between devices with their start and end apart: 4, of which 4 were waited for; matrix products, arithmetic and copies ran while one was open for 17% of the time, Pallas kernels for 0%

profile of v1, /device:TPU:1, one launch (start us, length us, event | category | flops | bytes accessed | tf_op | source)
XLA Modules:
  0.0 150.9 jit_solution(5236631825738464107)
XLA Ops:
  1.0 1.3 broadcast_select_fusion
  3.5 7.6 %all-to-all-start = ((bf16[8,16,1536]{2,0,1:T(8,128)(2,1)}), bf16[8,16,1536]{2,0,1:T(8,128)(2,1)S(1)}, u32[]{:S(2)}, u32[]{:S(2)}) async-start(bf16[8,16,1536]{2,0,1:T(8,128)(2,1)} %copy.30), calls=%async_computation | async-start | bytes 786432 | tf_op jit(solution)/shard_map/all_to_all | solution.py:79
  11.8 7.5 %all-to-all-done = bf16[8,16,1536]{2,0,1:T(8,128)(2,1)S(1)} async-done(((bf16[8,16,1536]{2,0,1:T(8,128)(2,1)}), bf16[8,16,1536]{2,0,1:T(8,128)(2,1)S(1)}, u32[]{:S(2)}, u32[]{:S(2)}) %all-to-all-start) | async-done | bytes 393248 | tf_op jit(solution)/shard_map/all_to_all | solution.py:79
  19.4 2.1 %convolution_convert_fusion = bf16[1536,128]{1,0:T(8,128)(2,1)} fusion(bf16[128,128]{1,0:T(8,128)(2,1)} %param.9, bf16[128,128]{1,0:T(8,128)(2,1)} %param.8, bf16[8,16,1536]{2,0,1:T(8,128)(2,1)S(1)} %all-to-all-done, f32[1536]{0:T(1024)S(1)} %fusion.52, f32[128]{0:T(128)} %param.10), kind=kOutput, calls=%fused_computation.13 | convolution fusion | flops 101842944 | bytes 858624 | tf_op jit(solution)/shard_map/dot_general | solution.py:61
  21.4 1.5 fusion.8
  22.9 4.5 %reshape.337 = bf16[64,4,3,16,8]{4,3,1,0,2:T(8,128)(2,1)} reshape(bf16[256,3,128]{2,0,1:T(8,128)(2,1)S(1)} %fusion.8) | data formatting | bytes 393216 | tf_op jit(solution)/shard_map/reshape | solution.py:91
  27.5 5.0 %copy.33 = bf16[16,64,4,3,8]{1,0,4,3,2:T(8,128)(2,1)S(1)} copy(bf16[16,64,4,3,8]{4,0,2,1,3:T(8,128)(2,1)} %bitcast.64) | data formatting | bytes 393216 | tf_op jit(solution)/shard_map/transpose | solution.py:92
  32.7 1.1 copy.34
  33.8 43.2 %all-to-all-start.1 = ((bf16[1024,1,96]{2,1,0:T(2,128)(2,1)}), bf16[1024,1,96]{2,1,0:T(2,128)(2,1)}, u32[]{:S(2)}, u32[]{:S(2)}) async-start(bf16[1024,1,96]{2,1,0:T(2,128)(2,1)} %copy.34), calls=%async_computation.1 | async-start | bytes 1048576 | tf_op jit(solution)/shard_map/all_to_all | solution.py:93
  77.0 1.1 fusion.43
  78.2 1.1 fusion.47
  79.3 7.7 %subtract_convert_fusion = (bf16[512,40,32]{2,1,0:T(8,128)(2,1)}, bf16[512,40,32]{2,1,0:T(8,128)(2,1)}) fusion(f32[512,32]{1,0:T(8,128)S(1)} %get-tuple-element.22, f32[512,40]{1,0:T(8,128)S(1)} %get-tuple-element.20, f32[512,32]{1,0:T(8,128)S(1)} %get-tuple-element.21, f32[512,40]{1,0:T(8,128)S(1)} %get-tuple-element.19), kind=kLoop, calls=%fused_computation.2 | loop fusion | flops 5898240 | bytes 2916352 | tf_op jit(solution)/shard_map/convert.3
  87.0 6.0 %neg.15 = bf16[64,8,1,1280]{3,1,0,2:T(8,128)(2,1)S(1)} reshape(bf16[512,40,32]{2,1,0:T(8,128)(2,1)} %get-tuple-element.6) | data formatting | bytes 2621440 | tf_op jit(solution)/shard_map/neg | solution.py:43
  93.0 1.3 copy.29
  94.3 6.0 %sub.39 = bf16[64,8,1,1280]{3,1,0,2:T(8,128)(2,1)S(1)} reshape(bf16[512,40,32]{2,1,0:T(8,128)(2,1)} %get-tuple-element.5) | data formatting | bytes 2621440 | tf_op jit(solution)/shard_map/sub | solution.py:41
  100.3 1.3 copy.28
  101.6 34.3 %all-to-all-done.1 = bf16[1024,1,96]{2,1,0:T(2,128)(2,1)} async-done(((bf16[1024,1,96]{2,1,0:T(2,128)(2,1)}), bf16[1024,1,96]{2,1,0:T(2,128)(2,1)}, u32[]{:S(2)}, u32[]{:S(2)}) %all-to-all-start.1) | async-done | bytes 196640 | tf_op jit(solution)/shard_map/all_to_all | solution.py:93
  136.0 1.2 copy.35
  137.6 2.3 %fusion.7 = f32[3,8,4,1280]{3,1,0,2:T(8,128)S(1)} fusion(bf16[64,8,1,1280]{3,0,1,2:T(8,128)(2,1)} %copy.29, bf16[64,8,1,1280]{3,0,1,2:T(8,128)(2,1)} %copy.28, bf16[4,64,8,3,2,8]{1,5,4,3,2,0:T(8,128)(2,1)S(1)} %bitcast.66), kind=kOutput, calls=%fused_computation.12 | convolution fusion | flops 257024000 | bytes 3309568 | tf_op jit(solution)/shard_map/twsfcl,wscx->fltx/dot_general | solution.py:98
  139.9 3.0 %collective-permute-start.1 = (f32[3,8,2,1280]{3,1,0,2:T(8,128)S(1)}, f32[3,8,2,1280]{3,1,0,2:T(8,128)S(1)}, u32[]{:S(2)}, u32[]{:S(2)}) collective-permute-start(f32[3,8,2,1280]{3,1,0,2:T(8,128)S(1)} %get-tuple-element.18), channel_id=1, source_target_pairs={{1,0},{2,1},{3,2},{4,3},{5,4},{6,5},{7,6},{8,7},{9,8},{10,9},{11,1... | collective-permute-start | bytes 737288 | tf_op jit(solution)/shard_map/ppermute | solution.py:22
  142.9 2.6 %collective-permute-start = (f32[3,8,2,1280]{3,1,0,2:T(8,128)S(1)}, f32[3,8,2,1280]{3,1,0,2:T(8,128)S(1)}, u32[]{:S(2)}, u32[]{:S(2)}) collective-permute-start(f32[3,8,2,1280]{3,1,0,2:T(8,128)S(1)} %get-tuple-element.17), channel_id=1, source_target_pairs={{0,1},{1,2},{2,3},{3,4},{4,5},{5,6},{6,7},{7,8},{8,9},{9,10},{10,1... | collective-permute-start | bytes 737288 | tf_op jit(solution)/shard_map/ppermute | solution.py:21
  145.6 1.8 %collective-permute-done.1 = f32[3,8,2,1280]{3,1,0,2:T(8,128)S(1)} collective-permute-done((f32[3,8,2,1280]{3,1,0,2:T(8,128)S(1)}, f32[3,8,2,1280]{3,1,0,2:T(8,128)S(1)}, u32[]{:S(2)}, u32[]{:S(2)}) %collective-permute-start.1) | collective-permute-done | bytes 245792 | tf_op jit(solution)/shard_map/ppermute | solution.py:22
  147.5 1.2 collective-permute-done
  150.0 1.0 copy.38
  (29 shorter events, 4.9 us)
Async XLA Ops:
  0.0 11.1 %copy-start = (bf16[8,512,256]{2,1,0:T(8,128)(2,1)S(1)}, bf16[8,512,256]{2,1,0:T(8,128)(2,1)}, u32[]{:S(2)}) copy-start(bf16[8,512,256]{2,1,0:T(8,128)(2,1)} %param.11) | copy-start | bytes 6291460
  3.5 15.8 %all-to-all-start = ((bf16[8,16,1536]{2,0,1:T(8,128)(2,1)}), bf16[8,16,1536]{2,0,1:T(8,128)(2,1)S(1)}, u32[]{:S(2)}, u32[]{:S(2)}) async-start(bf16[8,16,1536]{2,0,1:T(8,128)(2,1)} %copy.30), calls=%async_computation | async-start | bytes 786432 | tf_op jit(solution)/shard_map/all_to_all | solution.py:79
  21.4 55.6 %copy-start.1 = (s32[512]{0:T(512)S(1)}, s32[512]{0:T(512)}, u32[]{:S(2)}) copy-start(s32[512]{0:T(512)} %param.12) | copy-start | bytes 6148
  33.8 102.2 %all-to-all-start.1 = ((bf16[1024,1,96]{2,1,0:T(2,128)(2,1)}), bf16[1024,1,96]{2,1,0:T(2,128)(2,1)}, u32[]{:S(2)}, u32[]{:S(2)}) async-start(bf16[1024,1,96]{2,1,0:T(2,128)(2,1)} %copy.34), calls=%async_computation.1 | async-start | bytes 1048576 | tf_op jit(solution)/shard_map/all_to_all | solution.py:93
  137.6 7.9 %copy-start.2 = (s32[4]{0:T(128)S(1)}, s32[4]{0:T(128)}, u32[]{:S(2)}) copy-start(s32[4]{0:T(128)} %param.13) | copy-start | bytes 52
  139.9 7.5 %collective-permute-start.1 = (f32[3,8,2,1280]{3,1,0,2:T(8,128)S(1)}, f32[3,8,2,1280]{3,1,0,2:T(8,128)S(1)}, u32[]{:S(2)}, u32[]{:S(2)}) collective-permute-start(f32[3,8,2,1280]{3,1,0,2:T(8,128)S(1)} %get-tuple-element.18), channel_id=1, source_target_pairs={{1,0},{2,1},{3,2},{4,3},{5,4},{6,5},{7,6},{8,7},{9,8},{10,9},{11,1... | collective-permute-start | bytes 737288 | tf_op jit(solution)/shard_map/ppermute | solution.py:22
  142.9 5.7 %collective-permute-start = (f32[3,8,2,1280]{3,1,0,2:T(8,128)S(1)}, f32[3,8,2,1280]{3,1,0,2:T(8,128)S(1)}, u32[]{:S(2)}, u32[]{:S(2)}) collective-permute-start(f32[3,8,2,1280]{3,1,0,2:T(8,128)S(1)} %get-tuple-element.17), channel_id=1, source_target_pairs={{0,1},{1,2},{2,3},{3,4},{4,5},{5,6},{6,7},{7,8},{8,9},{9,10},{10,1... | collective-permute-start | bytes 737288 | tf_op jit(solution)/shard_map/ppermute | solution.py:21

commit v2 on v0

--- a/solution.py
+++ b/solution.py
@@ -63,13 +63,15 @@
     shard_count = lax.axis_size("wave")
     first_slot = lax.axis_index("wave") * wave_slots
     local_waves = lax.dynamic_slice_in_dim(wave_map, first_slot, wave_slots)
-    degrees = jnp.arange(degree_count, dtype=jnp.int32)
-    keep_mask = degrees[None, :] >= local_waves[:, None]
-    masked = jnp.where(keep_mask[None, :, None, None, :], spectral, jnp.zeros_like(spectral))
-    flattened = masked.reshape(lev_rows, -1)
+    flattened = spectral.reshape(lev_rows, -1)
     trig_rows = trig_table(wave_map, LON).reshape(shard_count, wave_slots, 2, LON)
     norm_factor = 1.0 / math.sqrt(wave_map.shape[0])
     columns = lax.all_to_all(flattened, "lev", split_axis=1, concat_axis=0, tiled=True)
+    column_count = columns.shape[1]
+    column_ids = lax.axis_index("lev") * column_count + jnp.arange(column_count, dtype=jnp.int32)
+    column_waves = jnp.take(local_waves, column_ids // (degree_count * field_count * 2))
+    keep_mask = column_ids % degree_count >= column_waves
+    columns = jnp.where(keep_mask[None, :], columns, jnp.zeros_like(columns))
     solved_cols = column_solve(columns, modes_in, modes_out, mode_depth, degree_count)
     group_count = solved_cols.shape[1] // degree_count
     group_ids = lax.axis_index("lev") * group_count + jnp.arange(group_count, dtype=jnp.int32)
@@ -87,12 +89,18 @@
         tiled=True,
     )
     lat_rows = arrived.shape[0]
-    split_bands = arrived.reshape(lat_rows, wave_slots, field_count, 2, shard_count, lev_rows)
-    grid_field = (
-        jnp.einsum("tsfcwl,wscx->fltx", split_bands, trig_rows, preferred_element_type=jnp.float32)
-        * norm_factor
-    )
-    wide_rows = with_halo(grid_field, (("wave", 2),), 2)
+
+    def synthesis(bands):
+        split_bands = bands.reshape(bands.shape[0], wave_slots, field_count, 2, shard_count, lev_rows)
+        return (
+            jnp.einsum("tsfcwl,wscx->fltx", split_bands, trig_rows, preferred_element_type=jnp.float32)
+            * norm_factor
+        )
+
+    band_halo = with_halo(arrived, (("wave", 0),), 2)
+    grid_field = synthesis(arrived)
+    halo_grid = synthesis(jnp.concatenate([band_halo[:2], band_halo[-2:]], axis=0))
+    wide_rows = jnp.concatenate([halo_grid[:, :, :2], grid_field, halo_grid[:, :, 2:]], axis=2)
     section_wide = wide_rows[:, :, 1:-1, :] - time_step * tendency(wide_rows)
     second = 0.5 * (grid_field + section_wide[:, :, 1:-1, :] - time_step * tendency(section_wide))
     points = jnp.arange(LON, dtype=jnp.int32)[None, :] < row_points[:, None]

time: 122 us -> 126 us (1.033)
  waiting for transfers between devices: 36.3 us -> 24.1 us
  local copies, waits for them, and re-layouts: 7.67 us -> 15.3 us
  other arithmetic: 15.3 us -> 19.1 us
  matrix products: 5.09 us -> 8.87 us
  blocking collectives: 10.2 us -> 13.1 us
  starting transfers between devices: 46.3 us -> 44.8 us
    all_to_all x1, waiting for transfers between devices: 7.54 us -> 0.93 us  [per_device(): lax.all_to_all(flattened, 'lev', split_axis=1, concat_axis=0, tiled=True)]
    reshape x0 -> x1, local copies, waits for them, and re-layouts: none -> 4.67 us  [synthesis(): bands.reshape(bands.shape[0], wave_slots, field_count, 2, shard_count, le...]
    gather x0 -> x2, other arithmetic: none -> 4.51 us  [per_device(): jnp.take(local_waves, column_ids // (degree_count * field_count * 2))]
    ppermute x1, waiting for transfers between devices: 4.4 us -> 0.01 us  [with_halo(): after = lax.ppermute(leading, axis, down)]
    dot_general x1 -> x2, matrix products: 2.31 us -> 6.06 us  [synthesis(): jnp.einsum('tsfcwl,wscx->fltx', split_bands, trig_rows, preferred_element...]
    all_to_all x1, blocking collectives: 10.2 us -> 13.1 us  [per_device(): lax.all_to_all(band_cols, 'lev', split_axis=2, concat_axis=1, tiled=True)]
    ppermute x1, starting transfers between devices: 1.92 us -> 3.54 us  [with_halo(): after = lax.ppermute(leading, axis, down)]
    ppermute x1, starting transfers between devices: 3.72 us -> 2.1 us  [with_halo(): before = lax.ppermute(last, axis, up)]
  transfers between devices with their start and end apart: 4 -> 4, of which waited for: 4 -> 2; matrix products, arithmetic and copies ran while one was open for 11% -> 19% of each run, Pallas kernels for 0% -> 0%
where the time goes in v2:
time: 126 us
  starting transfers between devices  44.8 us (36%)
  waiting for transfers between devices  24.1 us (19%)
  other arithmetic  19.1 us (15%)
  local copies, waits for them, and re-layouts  15.3 us (12%)
  blocking collectives  13.1 us (10%)
  matrix products  8.87 us (7%)
    all_to_all x1, starting transfers between devices, per_device(): lax.all_to_all(lax.all_to_all(band_cols, 'lev', split_axis=2, concat_axis...  31.6 us
    all_to_all x1, waiting for transfers between devices, per_device(): lax.all_to_all(lax.all_to_all(band_cols, 'lev', split_axis=2, concat_axis...  23.2 us
    all_to_all x1, blocking collectives, per_device(): lax.all_to_all(band_cols, 'lev', split_axis=2, concat_axis=1, tiled=True)  13.1 us
    another operation x1, other arithmetic  13.1 us
    all_to_all x1, starting transfers between devices, per_device(): lax.all_to_all(flattened, 'lev', split_axis=1, concat_axis=0, tiled=True)  7.57 us
    dot_general x2, matrix products, synthesis(): jnp.einsum('tsfcwl,wscx->fltx', split_bands, trig_rows, preferred_element...  6.06 us
    reshape x1, local copies, waits for them, and re-layouts, synthesis(): bands.reshape(bands.shape[0], wave_slots, field_count, 2, shard_count, le...  4.67 us
    gather x2, other arithmetic, per_device(): jnp.take(local_waves, column_ids // (degree_count * field_count * 2))  4.51 us
  transfers between devices with their start and end apart: 4, of which 2 were waited for; matrix products, arithmetic and copies ran while one was open for 19% of the time, Pallas kernels for 0%

profile of v2, /device:TPU:1, one launch (start us, length us, event | category | flops | bytes accessed | tf_op | source)
XLA Modules:
  0.0 125.5 jit_solution(15604388541614623064)
XLA Ops:
  0.0 1.4 %all_to_all.38 = bf16[8,16,1536]{2,1,0:T(8,128)(2,1)S(1)} reshape(bf16[8,8,3,2,512]{4,3,2,1,0:T(2,128)(2,1)} %param.7) | data formatting | bytes 786432 | tf_op jit(solution)/shard_map/all_to_all | solution.py:69
  1.4 1.0 copy.55
  2.4 7.6 %all-to-all-start = ((bf16[8,16,1536]{2,0,1:T(8,128)(2,1)}), bf16[8,16,1536]{2,0,1:T(8,128)(2,1)S(1)}, u32[]{:S(2)}, u32[]{:S(2)}) async-start(bf16[8,16,1536]{2,0,1:T(8,128)(2,1)} %copy.55), calls=%async_computation | async-start | bytes 786432 | tf_op jit(solution)/shard_map/all_to_all | solution.py:69
  10.0 0.8 dynamic_slice.3
  10.8 0.7 fusion.70
  11.5 0.6 gather_fusion
  12.2 4.4 %fusion.57 = s32[1536]{0:T(1024)S(1)} fusion(s32[]{:T(128)} %bitcast.2, s32[]{:T(128)} %bitcast.3, s32[]{:T(128)} %bitcast.4, s32[]{:T(128)} %bitcast.5, s32[]{:T(128)} %bitcast.6, s32[]{:T(128)} %bitcast.8, s32[]{:T(128)} %bitcast.7, s32[]{:T(128)S(6)} %mul.162), kind=kLoop, calls=%fused_computation.97 | loop fusion | flops 36864 | bytes 6176 | tf_op jit(solution)/shard_map/jit(_take)/gather | solution.py:72
  16.6 0.6 fusion.52
  17.3 0.9 all-to-all-done
  18.2 1.3 %convolution_convert_fusion = bf16[1536,128]{1,0:T(8,128)(2,1)} fusion(bf16[128,128]{1,0:T(8,128)(2,1)S(1)} %copy-done.3, bf16[128,128]{1,0:T(8,128)(2,1)S(1)} %copy-done.4, bf16[8,16,1536]{2,0,1:T(8,128)(2,1)S(1)} %all-to-all-done, f32[1536]{0:T(1024)S(1)} %fusion.51, f32[128]{0:T(128)S(1)} %copy-done.5, pred[1536]{0:T(1024)(128)(4,1)S(1)} %fusion.52), kind=kOutput, calls=%fused_computation.19 | convolution fusion | flops 102039552 | bytes 860160 | tf_op jit(solution)/shard_map/dot_general | solution.py:54
  19.5 1.5 %fusion.20 = bf16[256,3,128]{2,0,1:T(8,128)(2,1)S(1)} fusion(bf16[128,3,512]{0,2,1:T(8,128)(2,1)} %bitcast.94, bf16[3,512,256]{2,1,0:T(8,128)(2,1)S(1)} %gather_fusion, pred[3]{0:T(512)(128)(4,1)S(1)} %compare_and_fusion), kind=kOutput, calls=%fused_computation.24 | convolution fusion | flops 101154816 | bytes 1376259 | tf_op jit(solution)/shard_map/lgn,gnt->tgl/dot_general | solution.py:81
  21.2 13.1 %all_to_all.52 = bf16[256,3,128]{0,1,2:T(4,128)(2,1)S(1)} all-to-all(bf16[256,3,128]{0,1,2:T(4,128)(2,1)S(1)} %copy.58), channel_id=1, replica_groups=mesh['lev'=16,'wave'=64] {'lev'}, dimensions={2} | all-to-all | bytes 393216 | tf_op jit(solution)/shard_map/all_to_all | solution.py:85
  34.8 1.4 %reshape.299 = bf16[64,2,768]{2,1,0:T(2,128)(2,1)} reshape(bf16[256,8,48]{2,1,0:T(8,128)(2,1)S(1)} %bitcast.88) | data formatting | bytes 393216
  36.2 31.6 %all-to-all-start.2 = ((bf16[64,2,768]{2,1,0:T(2,128)(2,1)}), bf16[64,2,768]{2,1,0:T(2,128)(2,1)S(1)}, u32[]{:S(2)}, u32[]{:S(2)}) async-start(bf16[64,2,768]{2,1,0:T(2,128)(2,1)} %reshape.299), calls=%async_computation.2 | async-start | bytes 393216 | tf_op jit(solution)/shard_map/all_to_all | solution.py:84
  68.0 13.1 %cosine_convert_fusion = (bf16[64,8,1,1280]{3,0,1,2:T(8,128)(2,1)}, bf16[64,8,1,1280]{3,0,1,2:T(8,128)(2,1)}) fusion(s32[64,8]{0,1:T(8,128)S(1)} %copy.54), kind=kLoop, calls=%fused_computation.8 | loop fusion | flops 7864320 | bytes 2623488 | tf_op jit(solution)/shard_map/convert
  81.1 23.2 %all-to-all-done.2 = bf16[64,2,768]{2,1,0:T(2,128)(2,1)S(1)} async-done(((bf16[64,2,768]{2,1,0:T(2,128)(2,1)}), bf16[64,2,768]{2,1,0:T(2,128)(2,1)S(1)}, u32[]{:S(2)}, u32[]{:S(2)}) %all-to-all-start.2) | async-done | bytes 196640 | tf_op jit(solution)/shard_map/all_to_all | solution.py:84
  104.7 0.7 copy.62
  105.5 3.5 %collective-permute-start.1 = (bf16[2,48,512]{1,2,0:T(8,128)(2,1)S(1)}, bf16[2,48,512]{1,2,0:T(8,128)(2,1)}, u32[]{:S(2)}, u32[]{:S(2)}) collective-permute-start(bf16[2,48,512]{1,2,0:T(8,128)(2,1)S(1)} %bitcast.93), channel_id=1, source_target_pairs={{1,0},{2,1},{3,2},{4,3},{5,4},{6,5},{7,6},{8,7},{9,8},{10,9},{11,1... | collective-permute-start | bytes 294920 | tf_op jit(solution)/shard_map/ppermute | solution.py:22
  109.1 2.1 %collective-permute-start = (bf16[2,48,512]{1,2,0:T(8,128)(2,1)S(1)}, bf16[2,48,512]{1,2,0:T(8,128)(2,1)S(1)}, u32[]{:S(2)}, u32[]{:S(2)}) collective-permute-start(bf16[2,48,512]{1,2,0:T(8,128)(2,1)S(1)} %bitcast.92), channel_id=1, source_target_pairs={{0,1},{1,2},{2,3},{3,4},{4,5},{5,6},{6,7},{7,8},{8,9},{9,10},{10,1... | collective-permute-start | bytes 294920 | tf_op jit(solution)/shard_map/ppermute | solution.py:21
  111.2 2.3 %fusion.19 = f32[3,8,4,1280]{3,1,0,2:T(8,128)S(1)} fusion(bf16[64,8,1,1280]{3,0,1,2:T(8,128)(2,1)} %get-tuple-element.20, bf16[64,8,1,1280]{3,0,1,2:T(8,128)(2,1)} %get-tuple-element.19, bf16[4,8,3,2,64,8]{4,5,3,2,1,0:T(8,128)(2,1)S(1)} %bitcast.91), kind=kOutput, calls=%fused_computation.22 | convolution fusion | flops 257024000 | bytes 3309568 | tf_op jit(solution)/shard_map/tsfcwl,wscx->fltx/dot_general | solution.py:96
  113.5 1.1 copy.67
  114.7 4.7 %reshape.241 = bf16[4,8,3,2,64,8]{5,4,3,2,1,0:T(8,128)(2,1)} reshape(bf16[4,48,512]{2,1,0:T(8,128)(2,1)S(1)} %pad_maximum_fusion.5) | data formatting | bytes 393216 | tf_op jit(solution)/shard_map/reshape | solution.py:94
  119.4 3.8 %fusion.15 = f32[3,8,4,1280]{3,1,0,2:T(8,128)S(1)} fusion(bf16[4,8,3,2,64,8]{5,4,3,2,1,0:T(8,128)(2,1)} %reshape.241, bf16[64,8,1,1280]{3,0,1,2:T(8,128)(2,1)} %get-tuple-element.20, bf16[64,8,1,1280]{3,0,1,2:T(8,128)(2,1)} %get-tuple-element.19), kind=kOutput, calls=%fused_computation.18 | convolution fusion | flops 257024000 | bytes 3309568 | tf_op jit(solution)/shard_map/tsfcwl,wscx->fltx/dot_general | solution.py:96
  124.6 1.0 copy.69
  (41 shorter events, 3.1 us)
Async XLA Ops:
  0.0 11.5 %copy-start = (bf16[8,512,256]{2,1,0:T(8,128)(2,1)S(1)}, bf16[8,512,256]{2,1,0:T(8,128)(2,1)}, u32[]{:S(2)}) copy-start(bf16[8,512,256]{2,1,0:T(8,128)(2,1)} %param.11) | copy-start | bytes 6291460
  0.0 18.2 %copy-start.5 = (f32[128]{0:T(128)S(1)}, f32[128]{0:T(128)}, u32[]{:S(2)}) copy-start(f32[128]{0:T(128)} %param.10) | copy-start | bytes 1540
  0.0 18.2 %copy-start.3 = (bf16[128,128]{1,0:T(8,128)(2,1)S(1)}, bf16[128,128]{1,0:T(8,128)(2,1)}, u32[]{:S(2)}) copy-start(bf16[128,128]{1,0:T(8,128)(2,1)} %param.9) | copy-start | bytes 98308
  0.0 18.2 %copy-start.4 = (bf16[128,128]{1,0:T(8,128)(2,1)S(1)}, bf16[128,128]{1,0:T(8,128)(2,1)}, u32[]{:S(2)}) copy-start(bf16[128,128]{1,0:T(8,128)(2,1)} %param.8) | copy-start | bytes 98308
  2.4 15.8 %all-to-all-start = ((bf16[8,16,1536]{2,0,1:T(8,128)(2,1)}), bf16[8,16,1536]{2,0,1:T(8,128)(2,1)S(1)}, u32[]{:S(2)}, u32[]{:S(2)}) async-start(bf16[8,16,1536]{2,0,1:T(8,128)(2,1)} %copy.55), calls=%async_computation | async-start | bytes 786432 | tf_op jit(solution)/shard_map/all_to_all | solution.py:69
  19.5 48.2 %copy-start.1 = (s32[512]{0:T(512)S(1)}, s32[512]{0:T(512)}, u32[]{:S(2)}) copy-start(s32[512]{0:T(512)} %param.12) | copy-start | bytes 6148
  19.5 48.4 %copy-start.2 = (s32[4]{0:T(128)S(1)}, s32[4]{0:T(128)}, u32[]{:S(2)}) copy-start(s32[4]{0:T(128)} %param.13) | copy-start | bytes 52
  36.2 68.1 %all-to-all-start.2 = ((bf16[64,2,768]{2,1,0:T(2,128)(2,1)}), bf16[64,2,768]{2,1,0:T(2,128)(2,1)S(1)}, u32[]{:S(2)}, u32[]{:S(2)}) async-start(bf16[64,2,768]{2,1,0:T(2,128)(2,1)} %reshape.299), calls=%async_computation.2 | async-start | bytes 393216 | tf_op jit(solution)/shard_map/all_to_all | solution.py:84
  105.5 8.0 %collective-permute-start.1 = (bf16[2,48,512]{1,2,0:T(8,128)(2,1)S(1)}, bf16[2,48,512]{1,2,0:T(8,128)(2,1)}, u32[]{:S(2)}, u32[]{:S(2)}) collective-permute-start(bf16[2,48,512]{1,2,0:T(8,128)(2,1)S(1)} %bitcast.93), channel_id=1, source_target_pairs={{1,0},{2,1},{3,2},{4,3},{5,4},{6,5},{7,6},{8,7},{9,8},{10,9},{11,1... | collective-permute-start | bytes 294920 | tf_op jit(solution)/shard_map/ppermute | solution.py:22
  109.1 5.5 %collective-permute-start = (bf16[2,48,512]{1,2,0:T(8,128)(2,1)S(1)}, bf16[2,48,512]{1,2,0:T(8,128)(2,1)S(1)}, u32[]{:S(2)}, u32[]{:S(2)}) collective-permute-start(bf16[2,48,512]{1,2,0:T(8,128)(2,1)S(1)} %bitcast.92), channel_id=1, source_target_pairs={{0,1},{1,2},{2,3},{3,4},{4,5},{5,6},{6,7},{7,8},{8,9},{9,10},{10,1... | collective-permute-start | bytes 294920 | tf_op jit(solution)/shard_map/ppermute | solution.py:21

commit v3 on v2

--- a/solution.py
+++ b/solution.py
@@ -90,16 +90,20 @@
     )
     lat_rows = arrived.shape[0]
 
+    split_bands = arrived.reshape(lat_rows, wave_slots, field_count, 2, shard_count, lev_rows)
+
     def synthesis(bands):
-        split_bands = bands.reshape(bands.shape[0], wave_slots, field_count, 2, shard_count, lev_rows)
         return (
-            jnp.einsum("tsfcwl,wscx->fltx", split_bands, trig_rows, preferred_element_type=jnp.float32)
+            jnp.einsum("tsfcwl,wscx->fltx", bands, trig_rows, preferred_element_type=jnp.float32)
             * norm_factor
         )
 
-    band_halo = with_halo(arrived, (("wave", 0),), 2)
-    grid_field = synthesis(arrived)
-    halo_grid = synthesis(jnp.concatenate([band_halo[:2], band_halo[-2:]], axis=0))
+    up = [(i, i + 1) for i in range(shard_count - 1)]
+    down = [(j, i) for i, j in up]
+    before = lax.ppermute(split_bands[lat_rows - 2:], "wave", up)
+    after = lax.ppermute(split_bands[:2], "wave", down)
+    grid_field = synthesis(split_bands)
+    halo_grid = synthesis(jnp.concatenate([before, after], axis=0))
     wide_rows = jnp.concatenate([halo_grid[:, :, :2], grid_field, halo_grid[:, :, 2:]], axis=2)
     section_wide = wide_rows[:, :, 1:-1, :] - time_step * tendency(wide_rows)
     second = 0.5 * (grid_field + section_wide[:, :, 1:-1, :] - time_step * tendency(section_wide))

time: 126 us -> 121 us (0.960)
  local copies, waits for them, and re-layouts: 15.3 us -> 9.38 us
  waiting for transfers between devices: 24.1 us -> 27.4 us
  matrix products: 8.87 us -> 6.77 us
    reshape x1 -> x0, local copies, waits for them, and re-layouts: 4.67 us -> none  [synthesis(): bands.reshape(bands.shape[0], wave_slots, field_count, 2, shard_count, le...]
    ppermute x2, waiting for transfers between devices: 0.01 us -> 2.57 us  [the longest x1 2.57 us: per_device(): after = lax.ppermute(split_bands[:2], 'wave', down)]
    dot_general x2, matrix products: 6.06 us -> 3.99 us  [synthesis(): jnp.einsum('tsfcwl,wscx->fltx', bands, trig_rows, preferred_element_type=...]
  transfers between devices with their start and end apart: 4 -> 4, of which waited for: 2 -> 3; matrix products, arithmetic and copies ran while one was open for 19% -> 19% of each run, Pallas kernels for 0% -> 0%
where the time goes in v3:
time: 121 us; the launch traced here: 120 us
  starting transfers between devices  44.8 us (37%)
  waiting for transfers between devices  27.4 us (23%)
  other arithmetic  19.1 us (16%)
  blocking collectives  12.4 us (10%)
  local copies, waits for them, and re-layouts  9.38 us (8%)
  matrix products  6.77 us (6%)
    all_to_all x1, starting transfers between devices, per_device(): lax.all_to_all(lax.all_to_all(band_cols, 'lev', split_axis=2, concat_axis...  31.6 us
    all_to_all x1, waiting for transfers between devices, per_device(): lax.all_to_all(lax.all_to_all(band_cols, 'lev', split_axis=2, concat_axis...  23.2 us
    another operation x1, other arithmetic  13.1 us
    all_to_all x1, blocking collectives, per_device(): lax.all_to_all(band_cols, 'lev', split_axis=2, concat_axis=1, tiled=True)  12.4 us
    all_to_all x1, starting transfers between devices, per_device(): lax.all_to_all(flattened, 'lev', split_axis=1, concat_axis=0, tiled=True)  7.57 us
    gather x2, other arithmetic, per_device(): jnp.take(local_waves, column_ids // (degree_count * field_count * 2))  4.58 us
    dot_general x2, matrix products, synthesis(): jnp.einsum('tsfcwl,wscx->fltx', bands, trig_rows, preferred_element_type=...  3.99 us
    ppermute x1, starting transfers between devices, per_device(): before = lax.ppermute(split_bands[lat_rows - 2:], 'wave', up)  3.72 us
  transfers between devices with their start and end apart: 4, of which 3 were waited for; matrix products, arithmetic and copies ran while one was open for 19% of the time, Pallas kernels for 0%

profile of v3, /device:TPU:1, one launch (start us, length us, event | category | flops | bytes accessed | tf_op | source)
XLA Modules:
  0.0 120.1 jit_solution(14637581880680105380)
XLA Ops:
  0.0 1.4 %all_to_all.38 = bf16[8,16,1536]{2,1,0:T(8,128)(2,1)S(1)} reshape(bf16[8,8,3,2,512]{4,3,2,1,0:T(2,128)(2,1)} %param.7) | data formatting | bytes 786432 | tf_op jit(solution)/shard_map/all_to_all | solution.py:69
  1.4 1.0 copy.52
  2.4 7.6 %all-to-all-start = ((bf16[8,16,1536]{2,0,1:T(8,128)(2,1)}), bf16[8,16,1536]{2,0,1:T(8,128)(2,1)S(1)}, u32[]{:S(2)}, u32[]{:S(2)}) async-start(bf16[8,16,1536]{2,0,1:T(8,128)(2,1)} %copy.52), calls=%async_computation | async-start | bytes 786432 | tf_op jit(solution)/shard_map/all_to_all | solution.py:69
  10.1 0.7 fusion.64
  10.8 0.6 gather_fusion
  11.5 4.5 %fusion.51 = s32[1536]{0:T(1024)S(1)} fusion(s32[]{:T(128)} %bitcast.2, s32[]{:T(128)} %bitcast.3, s32[]{:T(128)} %bitcast.4, s32[]{:T(128)} %bitcast.5, s32[]{:T(128)} %bitcast.6, s32[]{:T(128)} %bitcast.8, s32[]{:T(128)} %bitcast.7, s32[]{:T(128)S(6)} %mul.162), kind=kLoop, calls=%fused_computation.95 | loop fusion | flops 36864 | bytes 6176 | tf_op jit(solution)/shard_map/jit(_take)/gather | solution.py:72
  16.0 0.6 fusion.46
  16.6 1.6 %all-to-all-done = bf16[8,16,1536]{2,0,1:T(8,128)(2,1)S(1)} async-done(((bf16[8,16,1536]{2,0,1:T(8,128)(2,1)}), bf16[8,16,1536]{2,0,1:T(8,128)(2,1)S(1)}, u32[]{:S(2)}, u32[]{:S(2)}) %all-to-all-start) | async-done | bytes 393248 | tf_op jit(solution)/shard_map/all_to_all | solution.py:69
  18.2 1.3 %convolution_convert_fusion = bf16[1536,128]{1,0:T(8,128)(2,1)} fusion(bf16[128,128]{1,0:T(8,128)(2,1)S(1)} %copy-done.5, bf16[128,128]{1,0:T(8,128)(2,1)S(1)} %copy-done.6, bf16[8,16,1536]{2,0,1:T(8,128)(2,1)S(1)} %all-to-all-done, f32[1536]{0:T(1024)S(1)} %fusion.45, f32[128]{0:T(128)S(1)} %copy-done.7, pred[1536]{0:T(1024)(128)(4,1)S(1)} %fusion.46), kind=kOutput, calls=%fused_computation.14 | convolution fusion | flops 102039552 | bytes 860160 | tf_op jit(solution)/shard_map/dot_general | solution.py:54
  19.5 1.5 %fusion.11 = bf16[256,3,128]{2,0,1:T(8,128)(2,1)S(1)} fusion(bf16[128,3,512]{0,2,1:T(8,128)(2,1)} %bitcast.90, bf16[3,512,256]{2,1,0:T(8,128)(2,1)S(1)} %gather_fusion, pred[3]{0:T(512)(128)(4,1)S(1)} %compare_and_fusion), kind=kOutput, calls=%fused_computation.22 | convolution fusion | flops 101154816 | bytes 1376259 | tf_op jit(solution)/shard_map/lgn,gnt->tgl/dot_general | solution.py:81
  21.2 12.4 %all_to_all.52 = bf16[256,3,128]{0,1,2:T(4,128)(2,1)S(1)} all-to-all(bf16[256,3,128]{0,1,2:T(4,128)(2,1)S(1)} %copy.55), channel_id=1, replica_groups=mesh['lev'=16,'wave'=64] {'lev'}, dimensions={2} | all-to-all | bytes 393216 | tf_op jit(solution)/shard_map/all_to_all | solution.py:85
  33.7 0.4 copy.58
  34.1 1.4 %reshape.295 = bf16[64,2,768]{2,1,0:T(2,128)(2,1)} reshape(bf16[256,8,48]{2,1,0:T(8,128)(2,1)S(1)} %bitcast.84) | data formatting | bytes 393216
  35.4 31.6 %all-to-all-start.2 = ((bf16[64,2,768]{2,1,0:T(2,128)(2,1)}), bf16[64,2,768]{2,1,0:T(2,128)(2,1)S(1)}, u32[]{:S(2)}, u32[]{:S(2)}) async-start(bf16[64,2,768]{2,1,0:T(2,128)(2,1)} %reshape.295), calls=%async_computation.2 | async-start | bytes 393216 | tf_op jit(solution)/shard_map/all_to_all | solution.py:84
  67.2 13.1 %cosine_convert_fusion = (bf16[64,8,1,1280]{3,0,1,2:T(8,128)(2,1)}, bf16[64,8,1,1280]{3,0,1,2:T(8,128)(2,1)}) fusion(s32[64,8]{0,1:T(8,128)S(1)} %copy.51), kind=kLoop, calls=%fused_computation.6 | loop fusion | flops 7864320 | bytes 2623488 | tf_op jit(solution)/shard_map/convert
  80.3 23.2 %all-to-all-done.2 = bf16[64,2,768]{2,1,0:T(2,128)(2,1)S(1)} async-done(((bf16[64,2,768]{2,1,0:T(2,128)(2,1)}), bf16[64,2,768]{2,1,0:T(2,128)(2,1)S(1)}, u32[]{:S(2)}, u32[]{:S(2)}) %all-to-all-start.2) | async-done | bytes 196640 | tf_op jit(solution)/shard_map/all_to_all | solution.py:84
  103.5 0.5 reshape.296
  104.0 0.7 copy.59
  105.1 3.7 %collective-permute-start = (bf16[2,8,3,2,64,8]{4,5,1,3,2,0:T(8,128)(2,1)S(1)}, bf16[2,8,3,2,64,8]{4,5,1,3,2,0:T(8,128)(2,1)}, u32[]{:S(2)}, u32[]{:S(2)}) collective-permute-start(bf16[2,8,3,2,64,8]{4,5,1,3,2,0:T(8,128)(2,1)S(1)} %copy.62), channel_id=1, source_target_pairs={{0,1},{1,2},{2,3},{3,4},{4,5},{5,6},{6,7},{7,8},{8,9},{9,10},{10,1... | collective-permute-start | bytes 294920 | tf_op jit(solution)/shard_map/ppermute | solution.py:103
  109.2 1.9 %collective-permute-start.1 = (bf16[2,8,3,2,64,8]{4,5,1,3,2,0:T(8,128)(2,1)S(1)}, bf16[2,8,3,2,64,8]{4,5,1,3,2,0:T(8,128)(2,1)S(1)}, u32[]{:S(2)}, u32[]{:S(2)}) collective-permute-start(bf16[2,8,3,2,64,8]{4,5,1,3,2,0:T(8,128)(2,1)S(1)} %copy.64), channel_id=1, source_target_pairs={{1,0},{2,1},{3,2},{4,3},{5,4},{6,5},{7,6},{8,7},{9,8},{10,9},{11,1... | collective-permute-start | bytes 294920 | tf_op jit(solution)/shard_map/ppermute | solution.py:104
  111.1 2.5 %fusion.10 = f32[3,8,4,1280]{3,1,0,2:T(8,128)S(1)} fusion(bf16[64,8,1,1280]{3,0,1,2:T(8,128)(2,1)} %get-tuple-element.20, bf16[64,8,1,1280]{3,0,1,2:T(8,128)(2,1)} %get-tuple-element.19, bf16[4,8,3,2,64,8]{4,5,3,2,1,0:T(8,128)(2,1)S(1)} %bitcast.89), kind=kOutput, calls=%fused_computation.20 | convolution fusion | flops 257024000 | bytes 3309568 | tf_op jit(solution)/shard_map/tsfcwl,wscx->fltx/dot_general | solution.py:97
  113.6 2.6 %collective-permute-done.1 = bf16[2,8,3,2,64,8]{4,5,1,3,2,0:T(8,128)(2,1)S(1)} collective-permute-done((bf16[2,8,3,2,64,8]{4,5,1,3,2,0:T(8,128)(2,1)S(1)}, bf16[2,8,3,2,64,8]{4,5,1,3,2,0:T(8,128)(2,1)S(1)}, u32[]{:S(2)}, u32[]{:S(2)}) %collective-permute-start.1) | collective-permute-done | bytes 98336 | tf_op jit(solution)/shard_map/ppermute | solution.py:104
  116.2 1.5 %fusion.8 = f32[3,8,4,1280]{3,1,0,2:T(8,128)S(1)} fusion(bf16[64,8,1,1280]{3,0,1,2:T(8,128)(2,1)S(1)} %copy-done.2, bf16[64,8,1,1280]{3,0,1,2:T(8,128)(2,1)S(1)} %copy-done.1, bf16[2,8,3,2,64,8]{4,5,1,3,2,0:T(8,128)(2,1)S(1)} %collective-permute-done.1, bf16[2,8,3,2,64,8]{4,5,1,3,2,0:T(8,128)(2,1)} %collective-permute-done), kind=kOutput, calls=%fused_computation.17 | convolution fusion | flops 257417216 | bytes 3309568 | tf_op jit(solution)/shard_map/tsfcwl,wscx->fltx/dot_general | solution.py:97
  119.1 1.0 copy.65
  (43 shorter events, 2.8 us)
Async XLA Ops:
  0.0 10.8 %copy-start = (bf16[8,512,256]{2,1,0:T(8,128)(2,1)S(1)}, bf16[8,512,256]{2,1,0:T(8,128)(2,1)}, u32[]{:S(2)}) copy-start(bf16[8,512,256]{2,1,0:T(8,128)(2,1)} %param.11) | copy-start | bytes 6291460
  0.0 10.0 %copy-start.3 = (s32[512]{0:T(512)S(1)}, s32[512]{0:T(512)}, u32[]{:S(2)}) copy-start(s32[512]{0:T(512)} %param.12) | copy-start | bytes 6148
  0.0 18.2 %copy-start.7 = (f32[128]{0:T(128)S(1)}, f32[128]{0:T(128)}, u32[]{:S(2)}) copy-start(f32[128]{0:T(128)} %param.10) | copy-start | bytes 1540
  0.0 18.2 %copy-start.6 = (bf16[128,128]{1,0:T(8,128)(2,1)S(1)}, bf16[128,128]{1,0:T(8,128)(2,1)}, u32[]{:S(2)}) copy-start(bf16[128,128]{1,0:T(8,128)(2,1)} %param.8) | copy-start | bytes 98308
  0.0 18.2 %copy-start.5 = (bf16[128,128]{1,0:T(8,128)(2,1)S(1)}, bf16[128,128]{1,0:T(8,128)(2,1)}, u32[]{:S(2)}) copy-start(bf16[128,128]{1,0:T(8,128)(2,1)} %param.9) | copy-start | bytes 98308
  2.4 15.8 %all-to-all-start = ((bf16[8,16,1536]{2,0,1:T(8,128)(2,1)}), bf16[8,16,1536]{2,0,1:T(8,128)(2,1)S(1)}, u32[]{:S(2)}, u32[]{:S(2)}) async-start(bf16[8,16,1536]{2,0,1:T(8,128)(2,1)} %copy.52), calls=%async_computation | async-start | bytes 786432 | tf_op jit(solution)/shard_map/all_to_all | solution.py:69
  21.0 46.1 %copy-start.4 = (s32[4]{0:T(128)S(1)}, s32[4]{0:T(128)}, u32[]{:S(2)}) copy-start(s32[4]{0:T(128)} %param.13) | copy-start | bytes 52
  35.4 68.1 %all-to-all-start.2 = ((bf16[64,2,768]{2,1,0:T(2,128)(2,1)}), bf16[64,2,768]{2,1,0:T(2,128)(2,1)S(1)}, u32[]{:S(2)}, u32[]{:S(2)}) async-start(bf16[64,2,768]{2,1,0:T(2,128)(2,1)} %reshape.295), calls=%async_computation.2 | async-start | bytes 393216 | tf_op jit(solution)/shard_map/all_to_all | solution.py:84
  105.1 8.5 %collective-permute-start = (bf16[2,8,3,2,64,8]{4,5,1,3,2,0:T(8,128)(2,1)S(1)}, bf16[2,8,3,2,64,8]{4,5,1,3,2,0:T(8,128)(2,1)}, u32[]{:S(2)}, u32[]{:S(2)}) collective-permute-start(bf16[2,8,3,2,64,8]{4,5,1,3,2,0:T(8,128)(2,1)S(1)} %copy.62), channel_id=1, source_target_pairs={{0,1},{1,2},{2,3},{3,4},{4,5},{5,6},{6,7},{7,8},{8,9},{9,10},{10,1... | collective-permute-start | bytes 294920 | tf_op jit(solution)/shard_map/ppermute | solution.py:103
  109.2 7.0 %collective-permute-start.1 = (bf16[2,8,3,2,64,8]{4,5,1,3,2,0:T(8,128)(2,1)S(1)}, bf16[2,8,3,2,64,8]{4,5,1,3,2,0:T(8,128)(2,1)S(1)}, u32[]{:S(2)}, u32[]{:S(2)}) collective-permute-start(bf16[2,8,3,2,64,8]{4,5,1,3,2,0:T(8,128)(2,1)S(1)} %copy.64), channel_id=1, source_target_pairs={{1,0},{2,1},{3,2},{4,3},{5,4},{6,5},{7,6},{8,7},{9,8},{10,9},{11,1... | collective-permute-start | bytes 294920 | tf_op jit(solution)/shard_map/ppermute | solution.py:104
  111.1 5.1 %copy-start.1 = (bf16[64,8,1,1280]{3,0,1,2:T(8,128)(2,1)S(1)}, bf16[64,8,1,1280]{3,0,1,2:T(8,128)(2,1)}, u32[]{:S(2)}) copy-start(bf16[64,8,1,1280]{3,0,1,2:T(8,128)(2,1)} %get-tuple-element.19) | copy-start | bytes 3932164
  111.1 5.1 %copy-start.2 = (bf16[64,8,1,1280]{3,0,1,2:T(8,128)(2,1)S(1)}, bf16[64,8,1,1280]{3,0,1,2:T(8,128)(2,1)}, u32[]{:S(2)}) copy-start(bf16[64,8,1,1280]{3,0,1,2:T(8,128)(2,1)} %get-tuple-element.20) | copy-start | bytes 3932164

commit v4 on v3

--- a/solution.py
+++ b/solution.py
@@ -3,7 +3,7 @@
 import jax
 import jax.numpy as jnp
 from jax import lax
-from jax.sharding import PartitionSpec as P
+from jax.sharding import Mesh, PartitionSpec as P
 
 LON = 1280
 
@@ -22,6 +22,18 @@
         after = lax.ppermute(leading, axis, down)
         value = jnp.concatenate([before, value, after], axis=dim)
     return value
+
+
+def lev_exchange(value, split_axis, concat_axis):
+    rows, cols = lax.axis_size("lev_y"), lax.axis_size("lev_x")
+    shape = value.shape
+    parts = value.reshape(*shape[:split_axis], rows, cols, shape[split_axis] // (rows * cols), *shape[split_axis + 1:])
+    parts = lax.all_to_all(parts, "lev_x", split_axis=split_axis + 1, concat_axis=concat_axis, tiled=True)
+    parts = lax.all_to_all(parts, "lev_y", split_axis=split_axis, concat_axis=concat_axis, tiled=True)
+    out_shape = list(shape)
+    out_shape[split_axis] //= rows * cols
+    out_shape[concat_axis] *= rows * cols
+    return parts.reshape(out_shape)
 
 
 def damping(mode_depth, degree_of, degree_total):
@@ -47,7 +59,7 @@
 
 def column_solve(columns, modes_in, modes_out, mode_depth, degree_count):
     column_count = columns.shape[1]
-    column_ids = lax.axis_index("lev") * column_count + jnp.arange(column_count, dtype=jnp.int32)
+    column_ids = lax.axis_index(("lev_y", "lev_x")) * column_count + jnp.arange(column_count, dtype=jnp.int32)
     degree_of = (column_ids % degree_count).astype(jnp.float32)
     modal_part = jnp.dot(modes_in, columns, preferred_element_type=jnp.float32)
     scaled = (modal_part * damping(mode_depth, degree_of, degree_count)).astype(jnp.bfloat16)
@@ -66,15 +78,15 @@
     flattened = spectral.reshape(lev_rows, -1)
     trig_rows = trig_table(wave_map, LON).reshape(shard_count, wave_slots, 2, LON)
     norm_factor = 1.0 / math.sqrt(wave_map.shape[0])
-    columns = lax.all_to_all(flattened, "lev", split_axis=1, concat_axis=0, tiled=True)
+    columns = lev_exchange(flattened, 1, 0)
     column_count = columns.shape[1]
-    column_ids = lax.axis_index("lev") * column_count + jnp.arange(column_count, dtype=jnp.int32)
+    column_ids = lax.axis_index(("lev_y", "lev_x")) * column_count + jnp.arange(column_count, dtype=jnp.int32)
     column_waves = jnp.take(local_waves, column_ids // (degree_count * field_count * 2))
     keep_mask = column_ids % degree_count >= column_waves
     columns = jnp.where(keep_mask[None, :], columns, jnp.zeros_like(columns))
     solved_cols = column_solve(columns, modes_in, modes_out, mode_depth, degree_count)
     group_count = solved_cols.shape[1] // degree_count
-    group_ids = lax.axis_index("lev") * group_count + jnp.arange(group_count, dtype=jnp.int32)
+    group_ids = lax.axis_index(("lev_y", "lev_x")) * group_count + jnp.arange(group_count, dtype=jnp.int32)
     slot_ids = group_ids // (field_count * 2)
     picked = jnp.take(legendre, slot_ids, axis=0)
     solved_groups = solved_cols.reshape(levels, group_count, degree_count)
@@ -82,7 +94,7 @@
         "lgn,gnt->tgl", solved_groups, picked, preferred_element_type=jnp.float32
     ).astype(jnp.bfloat16)
     arrived = lax.all_to_all(
-        lax.all_to_all(band_cols, "lev", split_axis=2, concat_axis=1, tiled=True),
+        lev_exchange(band_cols, 2, 1),
         "wave",
         split_axis=0,
         concat_axis=2,
@@ -112,8 +124,14 @@
 
 
 def solution(mesh):
+    lev_y = 4 if mesh.shape["lev"] % 4 == 0 else 1
+    split = Mesh(
+        mesh.devices.reshape(lev_y, mesh.shape["lev"] // lev_y, mesh.shape["wave"]),
+        ("lev_y", "lev_x", "wave"),
+    )
+    lev = ("lev_y", "lev_x")
     in_specs = (
-        P("lev", "wave", None, None, None),
+        P(lev, "wave", None, None, None),
         P(),
         P(),
         P(),
@@ -121,7 +139,7 @@
         P(),
         P("wave"),
     )
-    out_specs = P(None, "lev", "wave", None)
+    out_specs = P(None, lev, "wave", None)
     return jax.shard_map(
-        per_device, mesh=mesh, in_specs=in_specs, out_specs=out_specs, check_vma=False
+        per_device, mesh=split, in_specs=in_specs, out_specs=out_specs, check_vma=False
     )

time: 121 us -> 133 us (1.099)
  starting transfers between devices: 44.8 us -> 49.6 us
  waiting for transfers between devices: 27.4 us -> 31.6 us
  blocking collectives: 12.4 us -> 15.8 us
  matrix products: 6.77 us -> 4.93 us
    all_to_all x2 -> x3, starting transfers between devices: 39.1 us -> 44 us  [the longest x1 34.3 us: per_device(): lax.all_to_all(lev_exchange(band_cols, 2, 1), 'wave', split_axis=0, conca...]
    all_to_all x2 -> x3, waiting for transfers between devices: 24.8 us -> 29 us  [the longest x1 23.2 us: per_device(): lax.all_to_all(lev_exchange(band_cols, 2, 1), 'wave', split_axis=0, conca...]
    all_to_all x1 -> x2, blocking collectives: 12.4 us -> 15.8 us  [the longest x1 8.22 us: lev_exchange(): lax.all_to_all(parts, 'lev_x', split_axis=split_axis + 1, concat_axis=con...]
    another operation x0 -> x2, local copies, waits for them, and re-layouts: none -> 2.31 us  [lev_exchange(): value.reshape(*shape[:split_axis], rows, cols, shape[split_axis] // (rows...]
    all_to_all x6 -> x5, local copies, waits for them, and re-layouts: 3.45 us -> 1.54 us  [the longest x2 0.83 us: lev_exchange(): lax.all_to_all(parts, 'lev_x', split_axis=split_axis + 1, concat_axis=con...]
  transfers between devices with their start and end apart: 4 -> 5, of which waited for: 3 -> 4; matrix products, arithmetic and copies ran while one was open for 19% -> 17% of each run, Pallas kernels for 0% -> 0%
where the time goes in v4:
time: 133 us; the launch traced here: 132 us
  starting transfers between devices  49.6 us (37%)
  waiting for transfers between devices  31.6 us (24%)
  other arithmetic  19.9 us (15%)
  blocking collectives  15.8 us (12%)
  local copies, waits for them, and re-layouts  9.97 us (7%)
  matrix products  4.93 us (4%)
    all_to_all x1, starting transfers between devices, per_device(): lax.all_to_all(lev_exchange(band_cols, 2, 1), 'wave', split_axis=0, conca...  34.3 us
    all_to_all x1, waiting for transfers between devices, per_device(): lax.all_to_all(lev_exchange(band_cols, 2, 1), 'wave', split_axis=0, conca...  23.2 us
    another operation x1, other arithmetic  13.1 us
    all_to_all x1, blocking collectives, lev_exchange(): lax.all_to_all(parts, 'lev_x', split_axis=split_axis + 1, concat_axis=con...  8.22 us
    all_to_all x1, blocking collectives, lev_exchange(): lax.all_to_all(parts, 'lev_y', split_axis=split_axis, concat_axis=concat_...  7.54 us
    all_to_all x1, waiting for transfers between devices, lev_exchange(): lax.all_to_all(parts, 'lev_y', split_axis=split_axis, concat_axis=concat_...  5.5 us
    all_to_all x1, starting transfers between devices, lev_exchange(): lax.all_to_all(parts, 'lev_y', split_axis=split_axis, concat_axis=concat_...  4.87 us
    all_to_all x1, starting transfers between devices, lev_exchange(): lax.all_to_all(parts, 'lev_x', split_axis=split_axis + 1, concat_axis=con...  4.83 us
  transfers between devices with their start and end apart: 5, of which 4 were waited for; matrix products, arithmetic and copies ran while one was open for 17% of the time, Pallas kernels for 0%

profile of v4, /device:TPU:1, one launch (start us, length us, event | category | flops | bytes accessed | tf_op | source)
XLA Modules:
  0.0 132.0 jit_solution(7272782094244376212)
XLA Ops:
  0.0 1.4 %reshape_reshape.3 = bf16[8,4,4,1536]{3,2,1,0:T(4,128)(2,1)S(1)} reshape(bf16[8,8,3,2,512]{4,3,2,1,0:T(2,128)(2,1)} %param.7) | data formatting | bytes 786432 | tf_op jit(solution)/shard_map/reshape;reshape | solution.py:30
  1.4 0.9 copy.51
  2.3 4.8 %all-to-all-start = ((bf16[8,4,4,1536]{3,1,0,2:T(4,128)(2,1)}), bf16[8,4,4,1536]{3,1,0,2:T(4,128)(2,1)S(1)}, u32[]{:S(2)}, u32[]{:S(2)}) async-start(bf16[8,4,4,1536]{3,1,0,2:T(4,128)(2,1)} %copy.51), calls=%async_computation | async-start | bytes 786432 | tf_op jit(solution)/shard_map/all_to_all | solution.py:31
  8.0 0.7 fusion.57
  8.7 4.4 %fusion.46 = s32[1536]{0:T(1024)S(1)} fusion(s32[]{:T(128)} %bitcast.2, s32[]{:T(128)} %bitcast.3, s32[]{:T(128)} %bitcast.4, s32[]{:T(128)} %bitcast.5, s32[]{:T(128)} %bitcast.6, s32[]{:T(128)} %bitcast.8, s32[]{:T(128)} %bitcast.7, s32[]{:T(128)S(6)} %mul.168), kind=kLoop, calls=%fused_computation.93 | loop fusion | flops 36864 | bytes 6176 | tf_op jit(solution)/shard_map/jit(_take)/gather | solution.py:84
  13.4 0.8 copy.75
  14.2 4.9 %all-to-all-start.1 = ((bf16[32,4,1,1536]{3,0,2,1:T(8,128)(2,1)}), bf16[32,4,1,1536]{3,0,2,1:T(8,128)(2,1)S(1)}, u32[]{:S(2)}, u32[]{:S(2)}) async-start(bf16[32,4,1,1536]{3,0,2,1:T(8,128)(2,1)} %bitcast.96), calls=%async_computation.1 | async-start | bytes 786432 | tf_op jit(solution)/shard_map/all_to_all | solution.py:32
  19.1 0.7 fusion.41
  19.8 5.5 %all-to-all-done.1 = bf16[32,4,1,1536]{3,0,2,1:T(8,128)(2,1)S(1)} async-done(((bf16[32,4,1,1536]{3,0,2,1:T(8,128)(2,1)}), bf16[32,4,1,1536]{3,0,2,1:T(8,128)(2,1)S(1)}, u32[]{:S(2)}, u32[]{:S(2)}) %all-to-all-start.1) | async-done | bytes 393248 | tf_op jit(solution)/shard_map/all_to_all | solution.py:32
  25.3 0.8 bitcast_select_fusion
  26.1 1.5 %convolution_convert_fusion = bf16[1536,128]{1,0:T(8,128)(2,1)S(1)} fusion(bf16[128,128]{1,0:T(8,128)(2,1)S(1)} %copy-done.5, bf16[128,1536]{1,0:T(8,128)(2,1)} %bitcast_select_fusion, bf16[128,128]{1,0:T(8,128)(2,1)S(1)} %copy-done.6, f32[1536]{0:T(1024)S(1)} %fusion.40, f32[128]{0:T(128)S(1)} %copy-done.7), kind=kOutput, calls=%fused_computation.14 | convolution fusion | flops 101842944 | bytes 858624 | tf_op jit(solution)/shard_map/dot_general | solution.py:66
  28.0 8.2 %all_to_all.81 = bf16[256,3,4,4,8]{0,4,2,1,3:T(8,128)(2,1)S(1)} all-to-all(bf16[256,3,4,4,8]{0,4,2,1,3:T(8,128)(2,1)S(1)} %copy.55), channel_id=1, replica_groups=mesh['lev_y'=4,'lev_x'=4,'wave'=64] {'lev_x'}, dimensions={3} | all-to-all | bytes 393216 | tf_op jit(solution)/shard_map/all_to_all | solution.py:31
  36.3 7.5 %all_to_all.82 = bf16[256,12,4,1,8]{0,4,3,1,2:T(8,128)(2,1)S(1)} all-to-all(bf16[256,12,4,1,8]{0,4,3,1,2:T(8,128)(2,1)S(1)} %copy.56), channel_id=1, replica_groups=mesh['lev_y'=4,'lev_x'=4,'wave'=64] {'lev_y'}, dimensions={2} | all-to-all | bytes 393216 | tf_op jit(solution)/shard_map/all_to_all | solution.py:32
  44.2 1.4 %reshape.304 = bf16[64,2,768]{2,1,0:T(2,128)(2,1)} reshape(bf16[256,8,48]{2,1,0:T(8,128)(2,1)S(1)} %bitcast.100) | data formatting | bytes 393216
  45.6 34.3 %all-to-all-start.4 = ((bf16[64,2,768]{2,1,0:T(2,128)(2,1)}), bf16[64,2,768]{2,1,0:T(2,128)(2,1)S(1)}, u32[]{:S(2)}, u32[]{:S(2)}) async-start(bf16[64,2,768]{2,1,0:T(2,128)(2,1)} %reshape.304), calls=%async_computation.4 | async-start | bytes 393216 | tf_op jit(solution)/shard_map/all_to_all | solution.py:96
  80.1 13.1 %cosine_convert_fusion = (bf16[64,8,1,1280]{3,0,1,2:T(8,128)(2,1)}, bf16[64,8,1,1280]{3,0,1,2:T(8,128)(2,1)}) fusion(s32[64,8]{0,1:T(8,128)S(1)} %copy.50), kind=kLoop, calls=%fused_computation.6 | loop fusion | flops 7864320 | bytes 2623488 | tf_op jit(solution)/shard_map/convert
  93.2 23.2 %all-to-all-done.4 = bf16[64,2,768]{2,1,0:T(2,128)(2,1)S(1)} async-done(((bf16[64,2,768]{2,1,0:T(2,128)(2,1)}), bf16[64,2,768]{2,1,0:T(2,128)(2,1)S(1)}, u32[]{:S(2)}, u32[]{:S(2)}) %all-to-all-start.4) | async-done | bytes 196640 | tf_op jit(solution)/shard_map/all_to_all | solution.py:96
  116.9 0.7 copy.60
  118.0 3.7 %collective-permute-start = (bf16[2,8,3,2,64,8]{4,5,1,3,2,0:T(8,128)(2,1)S(1)}, bf16[2,8,3,2,64,8]{4,5,1,3,2,0:T(8,128)(2,1)S(1)}, u32[]{:S(2)}, u32[]{:S(2)}) collective-permute-start(bf16[2,8,3,2,64,8]{4,5,1,3,2,0:T(8,128)(2,1)S(1)} %copy.63), channel_id=1, source_target_pairs={{0,1},{1,2},{2,3},{3,4},{4,5},{5,6},{6,7},{7,8},{8,9},{9,10},{10,1... | collective-permute-start | bytes 294920 | tf_op jit(solution)/shard_map/ppermute | solution.py:115
  122.1 1.9 %collective-permute-start.1 = (bf16[2,8,3,2,64,8]{4,5,1,3,2,0:T(8,128)(2,1)S(1)}, bf16[2,8,3,2,64,8]{4,5,1,3,2,0:T(8,128)(2,1)S(1)}, u32[]{:S(2)}, u32[]{:S(2)}) collective-permute-start(bf16[2,8,3,2,64,8]{4,5,1,3,2,0:T(8,128)(2,1)S(1)} %copy.65), channel_id=1, source_target_pairs={{1,0},{2,1},{3,2},{4,3},{5,4},{6,5},{7,6},{8,7},{9,8},{10,9},{11,1... | collective-permute-start | bytes 294920 | tf_op jit(solution)/shard_map/ppermute | solution.py:116
  124.0 2.5 %fusion.10 = f32[3,8,4,1280]{3,1,0,2:T(8,128)S(1)} fusion(bf16[64,8,1,1280]{3,0,1,2:T(8,128)(2,1)} %get-tuple-element.20, bf16[64,8,1,1280]{3,0,1,2:T(8,128)(2,1)} %get-tuple-element.19, bf16[4,8,3,2,64,8]{4,5,3,2,1,0:T(8,128)(2,1)S(1)} %bitcast.106), kind=kOutput, calls=%fused_computation.20 | convolution fusion | flops 257024000 | bytes 3309568 | tf_op jit(solution)/shard_map/tsfcwl,wscx->fltx/dot_general | solution.py:109
  126.5 2.6 %collective-permute-done.1 = bf16[2,8,3,2,64,8]{4,5,1,3,2,0:T(8,128)(2,1)S(1)} collective-permute-done((bf16[2,8,3,2,64,8]{4,5,1,3,2,0:T(8,128)(2,1)S(1)}, bf16[2,8,3,2,64,8]{4,5,1,3,2,0:T(8,128)(2,1)S(1)}, u32[]{:S(2)}, u32[]{:S(2)}) %collective-permute-start.1) | collective-permute-done | bytes 98336 | tf_op jit(solution)/shard_map/ppermute | solution.py:116
  129.1 0.6 fusion.8
  131.0 1.0 copy.66
  (49 shorter events, 4.7 us)
Async XLA Ops:
  0.0 7.3 %copy-start = (bf16[8,512,256]{2,1,0:T(8,128)(2,1)S(1)}, bf16[8,512,256]{2,1,0:T(8,128)(2,1)}, u32[]{:S(2)}) copy-start(bf16[8,512,256]{2,1,0:T(8,128)(2,1)} %param.11) | copy-start | bytes 6291460
  0.0 7.2 %copy-start.3 = (s32[512]{0:T(512)S(1)}, s32[512]{0:T(512)}, u32[]{:S(2)}) copy-start(s32[512]{0:T(512)} %param.12) | copy-start | bytes 6148
  2.3 11.1 %all-to-all-start = ((bf16[8,4,4,1536]{3,1,0,2:T(4,128)(2,1)}), bf16[8,4,4,1536]{3,1,0,2:T(4,128)(2,1)S(1)}, u32[]{:S(2)}, u32[]{:S(2)}) async-start(bf16[8,4,4,1536]{3,1,0,2:T(4,128)(2,1)} %copy.51), calls=%async_computation | async-start | bytes 786432 | tf_op jit(solution)/shard_map/all_to_all | solution.py:31
  7.1 19.0 %copy-start.5 = (bf16[128,128]{1,0:T(8,128)(2,1)S(1)}, bf16[128,128]{1,0:T(8,128)(2,1)}, u32[]{:S(2)}) copy-start(bf16[128,128]{1,0:T(8,128)(2,1)} %param.9) | copy-start | bytes 98308
  7.1 19.0 %copy-start.6 = (bf16[128,128]{1,0:T(8,128)(2,1)S(1)}, bf16[128,128]{1,0:T(8,128)(2,1)}, u32[]{:S(2)}) copy-start(bf16[128,128]{1,0:T(8,128)(2,1)} %param.8) | copy-start | bytes 98308
  7.1 19.0 %copy-start.7 = (f32[128]{0:T(128)S(1)}, f32[128]{0:T(128)}, u32[]{:S(2)}) copy-start(f32[128]{0:T(128)} %param.10) | copy-start | bytes 1540
  14.2 11.1 %all-to-all-start.1 = ((bf16[32,4,1,1536]{3,0,2,1:T(8,128)(2,1)}), bf16[32,4,1,1536]{3,0,2,1:T(8,128)(2,1)S(1)}, u32[]{:S(2)}, u32[]{:S(2)}) async-start(bf16[32,4,1,1536]{3,0,2,1:T(8,128)(2,1)} %bitcast.96), calls=%async_computation.1 | async-start | bytes 786432 | tf_op jit(solution)/shard_map/all_to_all | solution.py:32
  28.0 52.0 %copy-start.4 = (s32[4]{0:T(128)S(1)}, s32[4]{0:T(128)}, u32[]{:S(2)}) copy-start(s32[4]{0:T(128)} %param.13) | copy-start | bytes 52
  45.6 70.8 %all-to-all-start.4 = ((bf16[64,2,768]{2,1,0:T(2,128)(2,1)}), bf16[64,2,768]{2,1,0:T(2,128)(2,1)S(1)}, u32[]{:S(2)}, u32[]{:S(2)}) async-start(bf16[64,2,768]{2,1,0:T(2,128)(2,1)} %reshape.304), calls=%async_computation.4 | async-start | bytes 393216 | tf_op jit(solution)/shard_map/all_to_all | solution.py:96
  118.0 8.5 %collective-permute-start = (bf16[2,8,3,2,64,8]{4,5,1,3,2,0:T(8,128)(2,1)S(1)}, bf16[2,8,3,2,64,8]{4,5,1,3,2,0:T(8,128)(2,1)S(1)}, u32[]{:S(2)}, u32[]{:S(2)}) collective-permute-start(bf16[2,8,3,2,64,8]{4,5,1,3,2,0:T(8,128)(2,1)S(1)} %copy.63), channel_id=1, source_target_pairs={{0,1},{1,2},{2,3},{3,4},{4,5},{5,6},{6,7},{7,8},{8,9},{9,10},{10,1... | collective-permute-start | bytes 294920 | tf_op jit(solution)/shard_map/ppermute | solution.py:115
  122.1 7.0 %collective-permute-start.1 = (bf16[2,8,3,2,64,8]{4,5,1,3,2,0:T(8,128)(2,1)S(1)}, bf16[2,8,3,2,64,8]{4,5,1,3,2,0:T(8,128)(2,1)S(1)}, u32[]{:S(2)}, u32[]{:S(2)}) collective-permute-start(bf16[2,8,3,2,64,8]{4,5,1,3,2,0:T(8,128)(2,1)S(1)} %copy.65), channel_id=1, source_target_pairs={{1,0},{2,1},{3,2},{4,3},{5,4},{6,5},{7,6},{8,7},{9,8},{10,9},{11,1... | collective-permute-start | bytes 294920 | tf_op jit(solution)/shard_map/ppermute | solution.py:116
  124.0 5.1 %copy-start.1 = (bf16[64,8,1,1280]{3,0,1,2:T(8,128)(2,1)S(1)}, bf16[64,8,1,1280]{3,0,1,2:T(8,128)(2,1)}, u32[]{:S(2)}) copy-start(bf16[64,8,1,1280]{3,0,1,2:T(8,128)(2,1)} %get-tuple-element.19) | copy-start | bytes 3932164
  124.0 5.1 %copy-start.2 = (bf16[64,8,1,1280]{3,0,1,2:T(8,128)(2,1)S(1)}, bf16[64,8,1,1280]{3,0,1,2:T(8,128)(2,1)}, u32[]{:S(2)}) copy-start(bf16[64,8,1,1280]{3,0,1,2:T(8,128)(2,1)} %get-tuple-element.20) | copy-start | bytes 3932164

commit v5 on v3

--- a/solution.py
+++ b/solution.py
@@ -93,8 +93,9 @@
     split_bands = arrived.reshape(lat_rows, wave_slots, field_count, 2, shard_count, lev_rows)
 
     def synthesis(bands):
+        ordered = bands.transpose(2, 5, 0, 1, 3, 4)
         return (
-            jnp.einsum("tsfcwl,wscx->fltx", bands, trig_rows, preferred_element_type=jnp.float32)
+            jnp.einsum("fltscw,wscx->fltx", ordered, trig_rows, preferred_element_type=jnp.float32)
             * norm_factor
         )
 

time: 121 us -> 123 us (1.017)
  other arithmetic: 19.1 us -> 22 us
where the time goes in v5:
time: 123 us
  starting transfers between devices  45 us (37%)
  waiting for transfers between devices  26.3 us (21%)
  other arithmetic  22 us (18%)
  blocking collectives  12.4 us (10%)
  local copies, waits for them, and re-layouts  8.95 us (7%)
  matrix products  7.64 us (6%)
    all_to_all x1, starting transfers between devices, per_device(): lax.all_to_all(lax.all_to_all(band_cols, 'lev', split_axis=2, concat_axis...  31.6 us
    all_to_all x1, waiting for transfers between devices, per_device(): lax.all_to_all(lax.all_to_all(band_cols, 'lev', split_axis=2, concat_axis...  23.2 us
    another operation x1, other arithmetic  13.1 us
    all_to_all x1, blocking collectives, per_device(): lax.all_to_all(band_cols, 'lev', split_axis=2, concat_axis=1, tiled=True)  12.4 us
    all_to_all x1, starting transfers between devices, per_device(): lax.all_to_all(flattened, 'lev', split_axis=1, concat_axis=0, tiled=True)  7.57 us
    dot_general x2, matrix products, synthesis(): jnp.einsum('fltscw,wscx->fltx', ordered, trig_rows, preferred_element_typ...  4.87 us
    gather x2, other arithmetic, per_device(): jnp.take(local_waves, column_ids // (degree_count * field_count * 2))  4.58 us
    ppermute x1, starting transfers between devices, per_device(): before = lax.ppermute(split_bands[lat_rows - 2:], 'wave', up)  3.72 us
  transfers between devices with their start and end apart: 4, of which 3 were waited for; matrix products, arithmetic and copies ran while one was open for 19% of the time, Pallas kernels for 0%

profile of v5, /device:TPU:1, one launch (start us, length us, event | category | flops | bytes accessed | tf_op | source)
XLA Modules:
  0.0 122.6 jit_solution(15469764096309205532)
XLA Ops:
  0.0 1.4 %all_to_all.38 = bf16[8,16,1536]{2,1,0:T(8,128)(2,1)S(1)} reshape(bf16[8,8,3,2,512]{4,3,2,1,0:T(2,128)(2,1)} %param.7) | data formatting | bytes 786432 | tf_op jit(solution)/shard_map/all_to_all | solution.py:69
  1.4 1.0 copy.52
  2.4 7.6 %all-to-all-start = ((bf16[8,16,1536]{2,0,1:T(8,128)(2,1)}), bf16[8,16,1536]{2,0,1:T(8,128)(2,1)S(1)}, u32[]{:S(2)}, u32[]{:S(2)}) async-start(bf16[8,16,1536]{2,0,1:T(8,128)(2,1)} %copy.52), calls=%async_computation | async-start | bytes 786432 | tf_op jit(solution)/shard_map/all_to_all | solution.py:69
  10.1 0.7 fusion.61
  10.8 0.6 gather_fusion
  11.5 4.5 %fusion.48 = s32[1536]{0:T(1024)S(1)} fusion(s32[]{:T(128)} %bitcast.2, s32[]{:T(128)} %bitcast.3, s32[]{:T(128)} %bitcast.4, s32[]{:T(128)} %bitcast.5, s32[]{:T(128)} %bitcast.6, s32[]{:T(128)} %bitcast.8, s32[]{:T(128)} %bitcast.7, s32[]{:T(128)S(6)} %mul.150), kind=kLoop, calls=%fused_computation.93 | loop fusion | flops 36864 | bytes 6176 | tf_op jit(solution)/shard_map/jit(_take)/gather | solution.py:72
  16.0 0.6 fusion.43
  16.6 1.6 %all-to-all-done = bf16[8,16,1536]{2,0,1:T(8,128)(2,1)S(1)} async-done(((bf16[8,16,1536]{2,0,1:T(8,128)(2,1)}), bf16[8,16,1536]{2,0,1:T(8,128)(2,1)S(1)}, u32[]{:S(2)}, u32[]{:S(2)}) %all-to-all-start) | async-done | bytes 393248 | tf_op jit(solution)/shard_map/all_to_all | solution.py:69
  18.2 1.3 %convolution_convert_fusion = bf16[1536,128]{1,0:T(8,128)(2,1)} fusion(bf16[128,128]{1,0:T(8,128)(2,1)S(1)} %copy-done.5, bf16[128,128]{1,0:T(8,128)(2,1)S(1)} %copy-done.6, bf16[8,16,1536]{2,0,1:T(8,128)(2,1)S(1)} %all-to-all-done, f32[1536]{0:T(1024)S(1)} %fusion.42, f32[128]{0:T(128)S(1)} %copy-done.7, pred[1536]{0:T(1024)(128)(4,1)S(1)} %fusion.43), kind=kOutput, calls=%fused_computation.18 | convolution fusion | flops 102039552 | bytes 860160 | tf_op jit(solution)/shard_map/dot_general | solution.py:54
  19.5 1.5 %fusion.9 = bf16[256,3,128]{2,0,1:T(8,128)(2,1)S(1)} fusion(bf16[128,3,512]{0,2,1:T(8,128)(2,1)} %bitcast.83, bf16[3,512,256]{2,1,0:T(8,128)(2,1)S(1)} %gather_fusion, pred[3]{0:T(512)(128)(4,1)S(1)} %compare_and_fusion), kind=kOutput, calls=%fused_computation.20 | convolution fusion | flops 101154816 | bytes 1376259 | tf_op jit(solution)/shard_map/lgn,gnt->tgl/dot_general | solution.py:81
  21.2 12.4 %all_to_all.52 = bf16[256,3,128]{0,1,2:T(4,128)(2,1)S(1)} all-to-all(bf16[256,3,128]{0,1,2:T(4,128)(2,1)S(1)} %copy.55), channel_id=1, replica_groups=mesh['lev'=16,'wave'=64] {'lev'}, dimensions={2} | all-to-all | bytes 393216 | tf_op jit(solution)/shard_map/all_to_all | solution.py:85
  34.1 1.4 %reshape.295 = bf16[64,2,768]{2,1,0:T(2,128)(2,1)} reshape(bf16[256,8,48]{2,1,0:T(8,128)(2,1)S(1)} %bitcast.77) | data formatting | bytes 393216
  35.4 31.6 %all-to-all-start.2 = ((bf16[64,2,768]{2,1,0:T(2,128)(2,1)}), bf16[64,2,768]{2,1,0:T(2,128)(2,1)S(1)}, u32[]{:S(2)}, u32[]{:S(2)}) async-start(bf16[64,2,768]{2,1,0:T(2,128)(2,1)} %reshape.295), calls=%async_computation.2 | async-start | bytes 393216 | tf_op jit(solution)/shard_map/all_to_all | solution.py:84
  67.2 13.1 %cosine_convert_fusion = (bf16[64,8,1,1280]{3,0,1,2:T(8,128)(2,1)}, bf16[64,8,1,1280]{3,0,1,2:T(8,128)(2,1)}) fusion(s32[64,8]{0,1:T(8,128)S(1)} %copy.61), kind=kLoop, calls=%fused_computation.6 | loop fusion | flops 7864320 | bytes 2623488 | tf_op jit(solution)/shard_map/convert
  80.3 23.2 %all-to-all-done.2 = bf16[64,2,768]{2,1,0:T(2,128)(2,1)S(1)} async-done(((bf16[64,2,768]{2,1,0:T(2,128)(2,1)}), bf16[64,2,768]{2,1,0:T(2,128)(2,1)S(1)}, u32[]{:S(2)}, u32[]{:S(2)}) %all-to-all-start.2) | async-done | bytes 196640 | tf_op jit(solution)/shard_map/all_to_all | solution.py:84
  104.0 0.7 copy.59
  105.1 3.7 %collective-permute-start = (bf16[2,8,3,2,64,8]{4,5,1,3,0,2:T(8,128)(2,1)S(1)}, bf16[2,8,3,2,64,8]{4,5,1,3,0,2:T(8,128)(2,1)}, u32[]{:S(2)}, u32[]{:S(2)}) collective-permute-start(bf16[2,8,3,2,64,8]{4,5,1,3,0,2:T(8,128)(2,1)S(1)} %copy.63), channel_id=1, source_target_pairs={{0,1},{1,2},{2,3},{3,4},{4,5},{5,6},{6,7},{7,8},{8,9},{9,10},{10,1... | collective-permute-start | bytes 294920 | tf_op jit(solution)/shard_map/ppermute | solution.py:104
  109.2 2.1 %collective-permute-start.1 = (bf16[2,8,3,2,64,8]{4,5,1,3,0,2:T(8,128)(2,1)S(1)}, bf16[2,8,3,2,64,8]{4,5,1,3,0,2:T(8,128)(2,1)S(1)}, u32[]{:S(2)}, u32[]{:S(2)}) collective-permute-start(bf16[2,8,3,2,64,8]{4,5,1,3,0,2:T(8,128)(2,1)S(1)} %copy.65), channel_id=1, source_target_pairs={{1,0},{2,1},{3,2},{4,3},{5,4},{6,5},{7,6},{8,7},{9,8},{10,9},{11,1... | collective-permute-start | bytes 294920 | tf_op jit(solution)/shard_map/ppermute | solution.py:105
  111.3 3.3 %fusion.8 = f32[3,8,4,1280]{3,2,1,0:T(4,128)S(1)} fusion(bf16[64,8,1,1280]{3,0,1,2:T(8,128)(2,1)} %get-tuple-element.20, bf16[64,8,1,1280]{3,0,1,2:T(8,128)(2,1)} %get-tuple-element.19, bf16[4,8,3,2,64,8]{4,5,3,2,1,0:T(8,128)(2,1)S(1)} %bitcast.82), kind=kOutput, calls=%fused_computation.17 | convolution fusion | flops 253091840 | bytes 3309568 | tf_op jit(solution)/shard_map/fltscw,wscx->fltx/dot_general | solution.py:98
  114.6 1.5 %collective-permute-done.1 = bf16[2,8,3,2,64,8]{4,5,1,3,0,2:T(8,128)(2,1)S(1)} collective-permute-done((bf16[2,8,3,2,64,8]{4,5,1,3,0,2:T(8,128)(2,1)S(1)}, bf16[2,8,3,2,64,8]{4,5,1,3,0,2:T(8,128)(2,1)S(1)}, u32[]{:S(2)}, u32[]{:S(2)}) %collective-permute-start.1) | collective-permute-done | bytes 98336 | tf_op jit(solution)/shard_map/ppermute | solution.py:105
  116.2 1.0 maximum_bitcast_fusion.3
  117.2 1.6 %fusion.7 = f32[3,8,4,1280]{3,2,1,0:T(4,128)S(1)} fusion(bf16[64,8,1,1280]{3,0,1,2:T(8,128)(2,1)S(1)} %copy-done.2, bf16[64,8,1,1280]{3,0,1,2:T(8,128)(2,1)S(1)} %copy-done.1, bf16[3,8,4,8,2,64]{5,1,3,4,2,0:T(8,128)(2,1)S(1)} %maximum_bitcast_fusion.3), kind=kOutput, calls=%fused_computation.15 | convolution fusion | flops 253091840 | bytes 3309568 | tf_op jit(solution)/shard_map/fltscw,wscx->fltx/dot_general | solution.py:98
  119.7 0.9 fusion.15
  121.2 1.4 %fusion.28 = f32[3,8,4,1280]{3,2,1,0:T(4,128)} fusion(f32[3,8,6,1280]{3,2,1,0:T(8,128)S(1)} %fusion.15, f32[3,8,4,1280]{3,2,1,0:T(4,128)S(1)} %fusion.8, f32[3,8,4,1]{3,2,1,0:T(4,128)S(1)} %get-tuple-element.8, f32[3,8,4,1279]{3,2,1,0:T(4,128)S(1)} %get-tuple-element.10, f32[3,8,4,1279]{3,2,1,0:T(4,128)S(1)} %get-tuple-element.9, ...), kind=kLoop, calls=%fused_computation.46 | loop fusion | flops 1474560 | bytes 3773440 | tf_op jit(solution)/shard_map/jit(_where)/select_n | solution.py:112
  (43 shorter events, 3.8 us)
Async XLA Ops:
  0.0 10.8 %copy-start = (bf16[8,512,256]{2,1,0:T(8,128)(2,1)S(1)}, bf16[8,512,256]{2,1,0:T(8,128)(2,1)}, u32[]{:S(2)}) copy-start(bf16[8,512,256]{2,1,0:T(8,128)(2,1)} %param.11) | copy-start | bytes 6291460
  0.0 10.0 %copy-start.3 = (s32[512]{0:T(512)S(1)}, s32[512]{0:T(512)}, u32[]{:S(2)}) copy-start(s32[512]{0:T(512)} %param.12) | copy-start | bytes 6148
  0.0 18.2 %copy-start.7 = (f32[128]{0:T(128)S(1)}, f32[128]{0:T(128)}, u32[]{:S(2)}) copy-start(f32[128]{0:T(128)} %param.10) | copy-start | bytes 1540
  0.0 18.2 %copy-start.6 = (bf16[128,128]{1,0:T(8,128)(2,1)S(1)}, bf16[128,128]{1,0:T(8,128)(2,1)}, u32[]{:S(2)}) copy-start(bf16[128,128]{1,0:T(8,128)(2,1)} %param.8) | copy-start | bytes 98308
  0.0 18.2 %copy-start.5 = (bf16[128,128]{1,0:T(8,128)(2,1)S(1)}, bf16[128,128]{1,0:T(8,128)(2,1)}, u32[]{:S(2)}) copy-start(bf16[128,128]{1,0:T(8,128)(2,1)} %param.9) | copy-start | bytes 98308
  2.4 15.8 %all-to-all-start = ((bf16[8,16,1536]{2,0,1:T(8,128)(2,1)}), bf16[8,16,1536]{2,0,1:T(8,128)(2,1)S(1)}, u32[]{:S(2)}, u32[]{:S(2)}) async-start(bf16[8,16,1536]{2,0,1:T(8,128)(2,1)} %copy.52), calls=%async_computation | async-start | bytes 786432 | tf_op jit(solution)/shard_map/all_to_all | solution.py:69
  21.0 46.1 %copy-start.4 = (s32[4]{0:T(128)S(1)}, s32[4]{0:T(128)}, u32[]{:S(2)}) copy-start(s32[4]{0:T(128)} %param.13) | copy-start | bytes 52
  35.4 68.1 %all-to-all-start.2 = ((bf16[64,2,768]{2,1,0:T(2,128)(2,1)}), bf16[64,2,768]{2,1,0:T(2,128)(2,1)S(1)}, u32[]{:S(2)}, u32[]{:S(2)}) async-start(bf16[64,2,768]{2,1,0:T(2,128)(2,1)} %reshape.295), calls=%async_computation.2 | async-start | bytes 393216 | tf_op jit(solution)/shard_map/all_to_all | solution.py:84
  105.1 9.5 %collective-permute-start = (bf16[2,8,3,2,64,8]{4,5,1,3,0,2:T(8,128)(2,1)S(1)}, bf16[2,8,3,2,64,8]{4,5,1,3,0,2:T(8,128)(2,1)}, u32[]{:S(2)}, u32[]{:S(2)}) collective-permute-start(bf16[2,8,3,2,64,8]{4,5,1,3,0,2:T(8,128)(2,1)S(1)} %copy.63), channel_id=1, source_target_pairs={{0,1},{1,2},{2,3},{3,4},{4,5},{5,6},{6,7},{7,8},{8,9},{9,10},{10,1... | collective-permute-start | bytes 294920 | tf_op jit(solution)/shard_map/ppermute | solution.py:104
  109.2 7.0 %collective-permute-start.1 = (bf16[2,8,3,2,64,8]{4,5,1,3,0,2:T(8,128)(2,1)S(1)}, bf16[2,8,3,2,64,8]{4,5,1,3,0,2:T(8,128)(2,1)S(1)}, u32[]{:S(2)}, u32[]{:S(2)}) collective-permute-start(bf16[2,8,3,2,64,8]{4,5,1,3,0,2:T(8,128)(2,1)S(1)} %copy.65), channel_id=1, source_target_pairs={{1,0},{2,1},{3,2},{4,3},{5,4},{6,5},{7,6},{8,7},{9,8},{10,9},{11,1... | collective-permute-start | bytes 294920 | tf_op jit(solution)/shard_map/ppermute | solution.py:105
  111.3 5.9 %copy-start.1 = (bf16[64,8,1,1280]{3,0,1,2:T(8,128)(2,1)S(1)}, bf16[64,8,1,1280]{3,0,1,2:T(8,128)(2,1)}, u32[]{:S(2)}) copy-start(bf16[64,8,1,1280]{3,0,1,2:T(8,128)(2,1)} %get-tuple-element.19) | copy-start | bytes 3932164
  111.3 5.9 %copy-start.2 = (bf16[64,8,1,1280]{3,0,1,2:T(8,128)(2,1)S(1)}, bf16[64,8,1,1280]{3,0,1,2:T(8,128)(2,1)}, u32[]{:S(2)}) copy-start(bf16[64,8,1,1280]{3,0,1,2:T(8,128)(2,1)} %get-tuple-element.20) | copy-start | bytes 3932164

commit v6 on v0

--- a/solution.py
+++ b/solution.py
@@ -63,13 +63,15 @@
     shard_count = lax.axis_size("wave")
     first_slot = lax.axis_index("wave") * wave_slots
     local_waves = lax.dynamic_slice_in_dim(wave_map, first_slot, wave_slots)
-    degrees = jnp.arange(degree_count, dtype=jnp.int32)
-    keep_mask = degrees[None, :] >= local_waves[:, None]
-    masked = jnp.where(keep_mask[None, :, None, None, :], spectral, jnp.zeros_like(spectral))
-    flattened = masked.reshape(lev_rows, -1)
+    flattened = spectral.reshape(lev_rows, -1)
     trig_rows = trig_table(wave_map, LON).reshape(shard_count, wave_slots, 2, LON)
     norm_factor = 1.0 / math.sqrt(wave_map.shape[0])
     columns = lax.all_to_all(flattened, "lev", split_axis=1, concat_axis=0, tiled=True)
+    column_count = columns.shape[1]
+    column_ids = lax.axis_index("lev") * column_count + jnp.arange(column_count, dtype=jnp.int32)
+    column_waves = jnp.take(local_waves, column_ids // (degree_count * field_count * 2))
+    keep_mask = column_ids % degree_count >= column_waves
+    columns = jnp.where(keep_mask[None, :], columns, jnp.zeros_like(columns))
     solved_cols = column_solve(columns, modes_in, modes_out, mode_depth, degree_count)
     group_count = solved_cols.shape[1] // degree_count
     group_ids = lax.axis_index("lev") * group_count + jnp.arange(group_count, dtype=jnp.int32)

time: 122 us -> 121 us (level)
  waiting for transfers between devices: 36.3 us -> 30.4 us
  other arithmetic: 15.3 us -> 19.1 us
  blocking collectives: 10.2 us -> 12.4 us
  starting transfers between devices: 46.3 us -> 44.8 us
    all_to_all x1, waiting for transfers between devices: 7.54 us -> 1.6 us  [per_device(): lax.all_to_all(flattened, 'lev', split_axis=1, concat_axis=0, tiled=True)]
    gather x0 -> x2, other arithmetic: none -> 4.51 us  [per_device(): jnp.take(local_waves, column_ids // (degree_count * field_count * 2))]
    all_to_all x1, blocking collectives: 10.2 us -> 12.4 us  [per_device(): lax.all_to_all(band_cols, 'lev', split_axis=2, concat_axis=1, tiled=True)]
    all_to_all x1, starting transfers between devices: 33.1 us -> 31.6 us  [per_device(): lax.all_to_all(lax.all_to_all(band_cols, 'lev', split_axis=2, concat_axis...]
    select_n x1 -> x0, other arithmetic: 1.32 us -> none  [per_device(): jnp.where(keep_mask[None, :, None, None, :], spectral, jnp.zeros_like(spe...]
  transfers between devices with their start and end apart: 4 -> 4, of which waited for: 4 -> 4; matrix products, arithmetic and copies ran while one was open for 11% -> 16% of each run, Pallas kernels for 0% -> 0%
where the time goes in v6:
time: 121 us
  starting transfers between devices  44.8 us (37%)
  waiting for transfers between devices  30.4 us (25%)
  other arithmetic  19.1 us (16%)
  blocking collectives  12.4 us (10%)
  local copies, waits for them, and re-layouts  8.66 us (7%)
  matrix products  5.1 us (4%)
    all_to_all x1, starting transfers between devices, per_device(): lax.all_to_all(lax.all_to_all(band_cols, 'lev', split_axis=2, concat_axis...  31.6 us
    all_to_all x1, waiting for transfers between devices, per_device(): lax.all_to_all(lax.all_to_all(band_cols, 'lev', split_axis=2, concat_axis...  23.3 us
    another operation x1, other arithmetic  13 us
    all_to_all x1, blocking collectives, per_device(): lax.all_to_all(band_cols, 'lev', split_axis=2, concat_axis=1, tiled=True)  12.4 us
    all_to_all x1, starting transfers between devices, per_device(): lax.all_to_all(flattened, 'lev', split_axis=1, concat_axis=0, tiled=True)  7.57 us
    gather x2, other arithmetic, per_device(): jnp.take(local_waves, column_ids // (degree_count * field_count * 2))  4.51 us
    ppermute x1, waiting for transfers between devices, with_halo(): after = lax.ppermute(leading, axis, down)  4.4 us
    ppermute x1, starting transfers between devices, with_halo(): before = lax.ppermute(last, axis, up)  3.72 us
  transfers between devices with their start and end apart: 4, of which 4 were waited for; matrix products, arithmetic and copies ran while one was open for 16% of the time, Pallas kernels for 0%

profile of v6, /device:TPU:1, one launch (start us, length us, event | category | flops | bytes accessed | tf_op | source)
XLA Modules:
  0.0 120.7 jit_solution(2318370995174107129)
XLA Ops:
  0.0 1.4 %all_to_all.38 = bf16[8,16,1536]{2,1,0:T(8,128)(2,1)S(1)} reshape(bf16[8,8,3,2,512]{4,3,2,1,0:T(2,128)(2,1)} %param.7) | data formatting | bytes 786432 | tf_op jit(solution)/shard_map/all_to_all | solution.py:69
  1.4 1.0 copy.42
  2.4 7.6 %all-to-all-start = ((bf16[8,16,1536]{2,0,1:T(8,128)(2,1)}), bf16[8,16,1536]{2,0,1:T(8,128)(2,1)S(1)}, u32[]{:S(2)}, u32[]{:S(2)}) async-start(bf16[8,16,1536]{2,0,1:T(8,128)(2,1)} %copy.42), calls=%async_computation | async-start | bytes 786432 | tf_op jit(solution)/shard_map/all_to_all | solution.py:69
  10.1 0.7 fusion.61
  10.8 0.6 gather_fusion
  11.5 4.4 %fusion.50 = s32[1536]{0:T(1024)S(1)} fusion(s32[]{:T(128)} %bitcast.2, s32[]{:T(128)} %bitcast.3, s32[]{:T(128)} %bitcast.4, s32[]{:T(128)} %bitcast.5, s32[]{:T(128)} %bitcast.6, s32[]{:T(128)} %bitcast.8, s32[]{:T(128)} %bitcast.7, s32[]{:T(128)S(6)} %mul.159), kind=kLoop, calls=%fused_computation.92 | loop fusion | flops 36864 | bytes 6176 | tf_op jit(solution)/shard_map/jit(_take)/gather | solution.py:72
  16.0 0.6 fusion.45
  16.6 1.6 %all-to-all-done = bf16[8,16,1536]{2,0,1:T(8,128)(2,1)S(1)} async-done(((bf16[8,16,1536]{2,0,1:T(8,128)(2,1)}), bf16[8,16,1536]{2,0,1:T(8,128)(2,1)S(1)}, u32[]{:S(2)}, u32[]{:S(2)}) %all-to-all-start) | async-done | bytes 393248 | tf_op jit(solution)/shard_map/all_to_all | solution.py:69
  18.2 1.3 %convolution_convert_fusion = bf16[1536,128]{1,0:T(8,128)(2,1)} fusion(bf16[128,128]{1,0:T(8,128)(2,1)S(1)} %copy-done.3, bf16[128,128]{1,0:T(8,128)(2,1)S(1)} %copy-done.4, bf16[8,16,1536]{2,0,1:T(8,128)(2,1)S(1)} %all-to-all-done, f32[1536]{0:T(1024)S(1)} %fusion.44, f32[128]{0:T(128)S(1)} %copy-done.5, pred[1536]{0:T(1024)(128)(4,1)S(1)} %fusion.45), kind=kOutput, calls=%fused_computation.20 | convolution fusion | flops 102039552 | bytes 860160 | tf_op jit(solution)/shard_map/dot_general | solution.py:54
  19.5 1.5 %fusion.13 = bf16[256,3,128]{2,0,1:T(8,128)(2,1)S(1)} fusion(bf16[128,3,512]{0,2,1:T(8,128)(2,1)} %bitcast.79, bf16[3,512,256]{2,1,0:T(8,128)(2,1)S(1)} %gather_fusion, pred[3]{0:T(512)(128)(4,1)S(1)} %compare_and_fusion), kind=kOutput, calls=%fused_computation.22 | convolution fusion | flops 101154816 | bytes 1376259 | tf_op jit(solution)/shard_map/lgn,gnt->tgl/dot_general | solution.py:81
  21.2 12.4 %all_to_all.52 = bf16[256,3,128]{0,1,2:T(4,128)(2,1)S(1)} all-to-all(bf16[256,3,128]{0,1,2:T(4,128)(2,1)S(1)} %copy.45), channel_id=1, replica_groups=mesh['lev'=16,'wave'=64] {'lev'}, dimensions={2} | all-to-all | bytes 393216 | tf_op jit(solution)/shard_map/all_to_all | solution.py:85
  34.1 1.4 %reshape.292 = bf16[64,2,768]{2,1,0:T(2,128)(2,1)} reshape(bf16[256,8,48]{2,1,0:T(8,128)(2,1)S(1)} %bitcast.75) | data formatting | bytes 393216
  35.5 31.6 %all-to-all-start.2 = ((bf16[64,2,768]{2,1,0:T(2,128)(2,1)}), bf16[64,2,768]{2,1,0:T(2,128)(2,1)S(1)}, u32[]{:S(2)}, u32[]{:S(2)}) async-start(bf16[64,2,768]{2,1,0:T(2,128)(2,1)} %reshape.292), calls=%async_computation.2 | async-start | bytes 393216 | tf_op jit(solution)/shard_map/all_to_all | solution.py:84
  67.2 13.0 %cosine_convert_fusion = (bf16[64,8,1,1280]{3,0,1,2:T(8,128)(2,1)}, bf16[64,8,1,1280]{3,0,1,2:T(8,128)(2,1)}) fusion(s32[64,8]{0,1:T(8,128)S(1)} %copy.41), kind=kLoop, calls=%fused_computation.9 | loop fusion | flops 7864320 | bytes 2623488 | tf_op jit(solution)/shard_map/convert
  80.2 23.3 %all-to-all-done.2 = bf16[64,2,768]{2,1,0:T(2,128)(2,1)S(1)} async-done(((bf16[64,2,768]{2,1,0:T(2,128)(2,1)}), bf16[64,2,768]{2,1,0:T(2,128)(2,1)S(1)}, u32[]{:S(2)}, u32[]{:S(2)}) %all-to-all-start.2) | async-done | bytes 196640 | tf_op jit(solution)/shard_map/all_to_all | solution.py:84
  103.5 0.5 reshape.293
  104.0 0.7 copy.49
  104.7 2.3 %fusion.12 = f32[3,8,4,1280]{3,1,0,2:T(8,128)S(1)} fusion(bf16[64,8,1,1280]{3,0,1,2:T(8,128)(2,1)} %get-tuple-element.18, bf16[64,8,1,1280]{3,0,1,2:T(8,128)(2,1)} %get-tuple-element.17, bf16[4,8,3,2,64,8]{4,5,3,2,1,0:T(8,128)(2,1)S(1)} %bitcast.78), kind=kOutput, calls=%fused_computation.19 | convolution fusion | flops 257024000 | bytes 3309568 | tf_op jit(solution)/shard_map/tsfcwl,wscx->fltx/dot_general | solution.py:94
  107.1 3.7 %collective-permute-start = (f32[3,8,2,1280]{3,1,0,2:T(8,128)S(1)}, f32[3,8,2,1280]{3,1,0,2:T(8,128)S(1)}, u32[]{:S(2)}, u32[]{:S(2)}) collective-permute-start(f32[3,8,2,1280]{3,1,0,2:T(8,128)S(1)} %get-tuple-element.15), channel_id=1, source_target_pairs={{0,1},{1,2},{2,3},{3,4},{4,5},{5,6},{6,7},{7,8},{8,9},{9,10},{10,1... | collective-permute-start | bytes 737288 | tf_op jit(solution)/shard_map/ppermute | solution.py:21
  110.8 1.9 %collective-permute-start.1 = (f32[3,8,2,1280]{3,1,0,2:T(8,128)S(1)}, f32[3,8,2,1280]{3,1,0,2:T(8,128)S(1)}, u32[]{:S(2)}, u32[]{:S(2)}) collective-permute-start(f32[3,8,2,1280]{3,1,0,2:T(8,128)S(1)} %get-tuple-element.16), channel_id=1, source_target_pairs={{1,0},{2,1},{3,2},{4,3},{5,4},{6,5},{7,6},{8,7},{9,8},{10,9},{11,1... | collective-permute-start | bytes 737288 | tf_op jit(solution)/shard_map/ppermute | solution.py:22
  112.8 1.1 collective-permute-done
  113.9 4.4 %collective-permute-done.1 = f32[3,8,2,1280]{3,1,0,2:T(8,128)S(1)} collective-permute-done((f32[3,8,2,1280]{3,1,0,2:T(8,128)S(1)}, f32[3,8,2,1280]{3,1,0,2:T(8,128)S(1)}, u32[]{:S(2)}, u32[]{:S(2)}) %collective-permute-start.1) | collective-permute-done | bytes 245792 | tf_op jit(solution)/shard_map/ppermute | solution.py:22
  118.7 0.4 fusion.24
  119.7 1.0 copy.51
  (33 shorter events, 2.1 us)
Async XLA Ops:
  0.0 10.8 %copy-start = (bf16[8,512,256]{2,1,0:T(8,128)(2,1)S(1)}, bf16[8,512,256]{2,1,0:T(8,128)(2,1)}, u32[]{:S(2)}) copy-start(bf16[8,512,256]{2,1,0:T(8,128)(2,1)} %param.11) | copy-start | bytes 6291460
  0.0 10.0 %copy-start.1 = (s32[512]{0:T(512)S(1)}, s32[512]{0:T(512)}, u32[]{:S(2)}) copy-start(s32[512]{0:T(512)} %param.12) | copy-start | bytes 6148
  0.0 18.2 %copy-start.5 = (f32[128]{0:T(128)S(1)}, f32[128]{0:T(128)}, u32[]{:S(2)}) copy-start(f32[128]{0:T(128)} %param.10) | copy-start | bytes 1540
  0.0 18.2 %copy-start.4 = (bf16[128,128]{1,0:T(8,128)(2,1)S(1)}, bf16[128,128]{1,0:T(8,128)(2,1)}, u32[]{:S(2)}) copy-start(bf16[128,128]{1,0:T(8,128)(2,1)} %param.8) | copy-start | bytes 98308
  0.0 18.2 %copy-start.3 = (bf16[128,128]{1,0:T(8,128)(2,1)S(1)}, bf16[128,128]{1,0:T(8,128)(2,1)}, u32[]{:S(2)}) copy-start(bf16[128,128]{1,0:T(8,128)(2,1)} %param.9) | copy-start | bytes 98308
  2.4 15.8 %all-to-all-start = ((bf16[8,16,1536]{2,0,1:T(8,128)(2,1)}), bf16[8,16,1536]{2,0,1:T(8,128)(2,1)S(1)}, u32[]{:S(2)}, u32[]{:S(2)}) async-start(bf16[8,16,1536]{2,0,1:T(8,128)(2,1)} %copy.42), calls=%async_computation | async-start | bytes 786432 | tf_op jit(solution)/shard_map/all_to_all | solution.py:69
  35.5 68.1 %all-to-all-start.2 = ((bf16[64,2,768]{2,1,0:T(2,128)(2,1)}), bf16[64,2,768]{2,1,0:T(2,128)(2,1)S(1)}, u32[]{:S(2)}, u32[]{:S(2)}) async-start(bf16[64,2,768]{2,1,0:T(2,128)(2,1)} %reshape.292), calls=%async_computation.2 | async-start | bytes 393216 | tf_op jit(solution)/shard_map/all_to_all | solution.py:84
  104.7 8.0 %copy-start.2 = (s32[4]{0:T(128)S(1)}, s32[4]{0:T(128)}, u32[]{:S(2)}) copy-start(s32[4]{0:T(128)} %param.13) | copy-start | bytes 52
  107.1 6.8 %collective-permute-start = (f32[3,8,2,1280]{3,1,0,2:T(8,128)S(1)}, f32[3,8,2,1280]{3,1,0,2:T(8,128)S(1)}, u32[]{:S(2)}, u32[]{:S(2)}) collective-permute-start(f32[3,8,2,1280]{3,1,0,2:T(8,128)S(1)} %get-tuple-element.15), channel_id=1, source_target_pairs={{0,1},{1,2},{2,3},{3,4},{4,5},{5,6},{6,7},{7,8},{8,9},{9,10},{10,1... | collective-permute-start | bytes 737288 | tf_op jit(solution)/shard_map/ppermute | solution.py:21
  110.8 7.5 %collective-permute-start.1 = (f32[3,8,2,1280]{3,1,0,2:T(8,128)S(1)}, f32[3,8,2,1280]{3,1,0,2:T(8,128)S(1)}, u32[]{:S(2)}, u32[]{:S(2)}) collective-permute-start(f32[3,8,2,1280]{3,1,0,2:T(8,128)S(1)} %get-tuple-element.16), channel_id=1, source_target_pairs={{1,0},{2,1},{3,2},{4,3},{5,4},{6,5},{7,6},{8,7},{9,8},{10,9},{11,1... | collective-permute-start | bytes 737288 | tf_op jit(solution)/shard_map/ppermute | solution.py:22

commit v7 on v3

--- a/solution.py
+++ b/solution.py
@@ -63,15 +63,13 @@
     shard_count = lax.axis_size("wave")
     first_slot = lax.axis_index("wave") * wave_slots
     local_waves = lax.dynamic_slice_in_dim(wave_map, first_slot, wave_slots)
-    flattened = spectral.reshape(lev_rows, -1)
+    degrees = jnp.arange(degree_count, dtype=jnp.int32)
+    keep_mask = degrees[None, :] >= local_waves[:, None]
+    masked = jnp.where(keep_mask[None, :, None, None, :], spectral, jnp.zeros_like(spectral))
+    flattened = masked.reshape(lev_rows, -1)
     trig_rows = trig_table(wave_map, LON).reshape(shard_count, wave_slots, 2, LON)
     norm_factor = 1.0 / math.sqrt(wave_map.shape[0])
     columns = lax.all_to_all(flattened, "lev", split_axis=1, concat_axis=0, tiled=True)
-    column_count = columns.shape[1]
-    column_ids = lax.axis_index("lev") * column_count + jnp.arange(column_count, dtype=jnp.int32)
-    column_waves = jnp.take(local_waves, column_ids // (degree_count * field_count * 2))
-    keep_mask = column_ids % degree_count >= column_waves
-    columns = jnp.where(keep_mask[None, :], columns, jnp.zeros_like(columns))
     solved_cols = column_solve(columns, modes_in, modes_out, mode_depth, degree_count)
     group_count = solved_cols.shape[1] // degree_count
     group_ids = lax.axis_index("lev") * group_count + jnp.arange(group_count, dtype=jnp.int32)

time: 121 us -> 121 us (level)
  waiting for transfers between devices: 27.4 us -> 33.3 us
  other arithmetic: 19.1 us -> 15.3 us
  blocking collectives: 12.4 us -> 10.2 us
  starting transfers between devices: 44.8 us -> 46.3 us
    all_to_all x1, waiting for transfers between devices: 1.61 us -> 7.54 us  [per_device(): lax.all_to_all(flattened, 'lev', split_axis=1, concat_axis=0, tiled=True)]
    gather x2 -> x0, other arithmetic: 4.58 us -> none  [per_device(): jnp.take(local_waves, column_ids // (degree_count * field_count * 2))]
    all_to_all x1, blocking collectives: 12.4 us -> 10.2 us  [per_device(): lax.all_to_all(band_cols, 'lev', split_axis=2, concat_axis=1, tiled=True)]
    all_to_all x1, starting transfers between devices: 31.6 us -> 33.1 us  [per_device(): lax.all_to_all(lax.all_to_all(band_cols, 'lev', split_axis=2, concat_axis...]
    select_n x0 -> x1, other arithmetic: none -> 1.32 us  [per_device(): jnp.where(keep_mask[None, :, None, None, :], spectral, jnp.zeros_like(spe...]
  transfers between devices with their start and end apart: 4 -> 4, of which waited for: 3 -> 3; matrix products, arithmetic and copies ran while one was open for 19% -> 14% of each run, Pallas kernels for 0% -> 0%
where the time goes in v7:
time: 121 us
  starting transfers between devices  46.3 us (38%)
  waiting for transfers between devices  33.3 us (28%)
  other arithmetic  15.3 us (13%)
  blocking collectives  10.2 us (8%)
  local copies, waits for them, and re-layouts  8.39 us (7%)
  matrix products  6.76 us (6%)
    all_to_all x1, starting transfers between devices, per_device(): lax.all_to_all(lax.all_to_all(band_cols, 'lev', split_axis=2, concat_axis...  33.1 us
    all_to_all x1, waiting for transfers between devices, per_device(): lax.all_to_all(lax.all_to_all(band_cols, 'lev', split_axis=2, concat_axis...  23.2 us
    another operation x1, other arithmetic  13.1 us
    all_to_all x1, blocking collectives, per_device(): lax.all_to_all(band_cols, 'lev', split_axis=2, concat_axis=1, tiled=True)  10.2 us
    all_to_all x1, starting transfers between devices, per_device(): lax.all_to_all(flattened, 'lev', split_axis=1, concat_axis=0, tiled=True)  7.57 us
    all_to_all x1, waiting for transfers between devices, per_device(): lax.all_to_all(flattened, 'lev', split_axis=1, concat_axis=0, tiled=True)  7.54 us
    dot_general x2, matrix products, synthesis(): jnp.einsum('tsfcwl,wscx->fltx', bands, trig_rows, preferred_element_type=...  3.99 us
    ppermute x1, starting transfers between devices, per_device(): before = lax.ppermute(split_bands[lat_rows - 2:], 'wave', up)  3.72 us
  transfers between devices with their start and end apart: 4, of which 3 were waited for; matrix products, arithmetic and copies ran while one was open for 14% of the time, Pallas kernels for 0%

profile of v7, /device:TPU:1, one launch (start us, length us, event | category | flops | bytes accessed | tf_op | source)
XLA Modules:
  0.0 120.6 jit_solution(15066846362418690527)
XLA Ops:
  0.0 0.9 dynamic_slice.3
  1.0 1.3 %broadcast_select_fusion = bf16[8,8,3,2,512]{4,3,2,1,0:T(2,128)(2,1)S(1)} fusion(bf16[8,8,3,2,512]{4,3,2,1,0:T(2,128)(2,1)} %param.7, pred[8,512]{1,0:T(8,128)(4,1)S(1)} %iota_compare_fusion.1), kind=kLoop, calls=%fused_computation.29 | loop fusion | flops 196608 | bytes 790528 | tf_op jit(solution)/shard_map/jit(_where)/select_n | solution.py:68
  2.6 1.0 copy.52
  3.6 7.6 %all-to-all-start = ((bf16[8,16,1536]{2,0,1:T(8,128)(2,1)}), bf16[8,16,1536]{2,0,1:T(8,128)(2,1)S(1)}, u32[]{:S(2)}, u32[]{:S(2)}) async-start(bf16[8,16,1536]{2,0,1:T(8,128)(2,1)} %copy.52), calls=%async_computation | async-start | bytes 786432 | tf_op jit(solution)/shard_map/all_to_all | solution.py:72
  11.2 0.6 gather_fusion
  11.8 7.5 %all-to-all-done = bf16[8,16,1536]{2,0,1:T(8,128)(2,1)S(1)} async-done(((bf16[8,16,1536]{2,0,1:T(8,128)(2,1)}), bf16[8,16,1536]{2,0,1:T(8,128)(2,1)S(1)}, u32[]{:S(2)}, u32[]{:S(2)}) %all-to-all-start) | async-done | bytes 393248 | tf_op jit(solution)/shard_map/all_to_all | solution.py:72
  19.4 1.3 %convolution_convert_fusion = bf16[1536,128]{1,0:T(8,128)(2,1)} fusion(bf16[128,128]{1,0:T(8,128)(2,1)S(1)} %copy-done.5, bf16[128,128]{1,0:T(8,128)(2,1)S(1)} %copy-done.6, bf16[8,16,1536]{2,0,1:T(8,128)(2,1)S(1)} %all-to-all-done, f32[1536]{0:T(1024)S(1)} %fusion.44, f32[128]{0:T(128)S(1)} %copy-done.7), kind=kOutput, calls=%fused_computation.14 | convolution fusion | flops 101842944 | bytes 858624 | tf_op jit(solution)/shard_map/dot_general | solution.py:54
  20.7 1.5 %fusion.11 = bf16[256,3,128]{2,0,1:T(8,128)(2,1)S(1)} fusion(bf16[128,3,512]{0,2,1:T(8,128)(2,1)} %bitcast.82, bf16[3,512,256]{2,1,0:T(8,128)(2,1)S(1)} %gather_fusion, pred[3]{0:T(512)(128)(4,1)S(1)} %compare_and_fusion), kind=kOutput, calls=%fused_computation.22 | convolution fusion | flops 101154816 | bytes 1376259 | tf_op jit(solution)/shard_map/lgn,gnt->tgl/dot_general | solution.py:79
  22.4 10.2 %all_to_all.52 = bf16[256,3,128]{0,1,2:T(4,128)(2,1)S(1)} all-to-all(bf16[256,3,128]{0,1,2:T(4,128)(2,1)S(1)} %copy.55), channel_id=1, replica_groups=mesh['lev'=16,'wave'=64] {'lev'}, dimensions={2} | all-to-all | bytes 393216 | tf_op jit(solution)/shard_map/all_to_all | solution.py:83
  32.6 0.4 copy.58
  33.0 1.4 %reshape.202 = bf16[64,2,768]{2,1,0:T(2,128)(2,1)} reshape(bf16[256,8,48]{2,1,0:T(8,128)(2,1)S(1)} %bitcast.76) | data formatting | bytes 393216
  34.4 33.1 %all-to-all-start.2 = ((bf16[64,2,768]{2,1,0:T(2,128)(2,1)}), bf16[64,2,768]{2,1,0:T(2,128)(2,1)S(1)}, u32[]{:S(2)}, u32[]{:S(2)}) async-start(bf16[64,2,768]{2,1,0:T(2,128)(2,1)} %reshape.202), calls=%async_computation.2 | async-start | bytes 393216 | tf_op jit(solution)/shard_map/all_to_all | solution.py:82
  67.7 13.1 %cosine_convert_fusion = (bf16[64,8,1,1280]{3,0,1,2:T(8,128)(2,1)}, bf16[64,8,1,1280]{3,0,1,2:T(8,128)(2,1)}) fusion(s32[64,8]{0,1:T(8,128)S(1)} %copy.51), kind=kLoop, calls=%fused_computation.6 | loop fusion | flops 7864320 | bytes 2623488 | tf_op jit(solution)/shard_map/convert
  80.8 23.2 %all-to-all-done.2 = bf16[64,2,768]{2,1,0:T(2,128)(2,1)S(1)} async-done(((bf16[64,2,768]{2,1,0:T(2,128)(2,1)}), bf16[64,2,768]{2,1,0:T(2,128)(2,1)S(1)}, u32[]{:S(2)}, u32[]{:S(2)}) %all-to-all-start.2) | async-done | bytes 196640 | tf_op jit(solution)/shard_map/all_to_all | solution.py:82
  104.0 0.5 reshape.203
  104.5 0.7 copy.59
  105.6 3.7 %collective-permute-start = (bf16[2,8,3,2,64,8]{4,5,1,3,2,0:T(8,128)(2,1)S(1)}, bf16[2,8,3,2,64,8]{4,5,1,3,2,0:T(8,128)(2,1)}, u32[]{:S(2)}, u32[]{:S(2)}) collective-permute-start(bf16[2,8,3,2,64,8]{4,5,1,3,2,0:T(8,128)(2,1)S(1)} %copy.62), channel_id=1, source_target_pairs={{0,1},{1,2},{2,3},{3,4},{4,5},{5,6},{6,7},{7,8},{8,9},{9,10},{10,1... | collective-permute-start | bytes 294920 | tf_op jit(solution)/shard_map/ppermute | solution.py:101
  109.3 0.3 copy.63
  109.7 1.9 %collective-permute-start.1 = (bf16[2,8,3,2,64,8]{4,5,1,3,2,0:T(8,128)(2,1)S(1)}, bf16[2,8,3,2,64,8]{4,5,1,3,2,0:T(8,128)(2,1)S(1)}, u32[]{:S(2)}, u32[]{:S(2)}) collective-permute-start(bf16[2,8,3,2,64,8]{4,5,1,3,2,0:T(8,128)(2,1)S(1)} %copy.64), channel_id=1, source_target_pairs={{1,0},{2,1},{3,2},{4,3},{5,4},{6,5},{7,6},{8,7},{9,8},{10,9},{11,1... | collective-permute-start | bytes 294920 | tf_op jit(solution)/shard_map/ppermute | solution.py:102
  111.6 2.5 %fusion.10 = f32[3,8,4,1280]{3,1,0,2:T(8,128)S(1)} fusion(bf16[64,8,1,1280]{3,0,1,2:T(8,128)(2,1)} %get-tuple-element.20, bf16[64,8,1,1280]{3,0,1,2:T(8,128)(2,1)} %get-tuple-element.19, bf16[4,8,3,2,64,8]{4,5,3,2,1,0:T(8,128)(2,1)S(1)} %bitcast.81), kind=kOutput, calls=%fused_computation.20 | convolution fusion | flops 257024000 | bytes 3309568 | tf_op jit(solution)/shard_map/tsfcwl,wscx->fltx/dot_general | solution.py:95
  114.1 2.6 %collective-permute-done.1 = bf16[2,8,3,2,64,8]{4,5,1,3,2,0:T(8,128)(2,1)S(1)} collective-permute-done((bf16[2,8,3,2,64,8]{4,5,1,3,2,0:T(8,128)(2,1)S(1)}, bf16[2,8,3,2,64,8]{4,5,1,3,2,0:T(8,128)(2,1)S(1)}, u32[]{:S(2)}, u32[]{:S(2)}) %collective-permute-start.1) | collective-permute-done | bytes 98336 | tf_op jit(solution)/shard_map/ppermute | solution.py:102
  116.7 1.5 %fusion.8 = f32[3,8,4,1280]{3,1,0,2:T(8,128)S(1)} fusion(bf16[64,8,1,1280]{3,0,1,2:T(8,128)(2,1)S(1)} %copy-done.2, bf16[64,8,1,1280]{3,0,1,2:T(8,128)(2,1)S(1)} %copy-done.1, bf16[2,8,3,2,64,8]{4,5,1,3,2,0:T(8,128)(2,1)S(1)} %collective-permute-done.1, bf16[2,8,3,2,64,8]{4,5,1,3,2,0:T(8,128)(2,1)} %collective-permute-done), kind=kOutput, calls=%fused_computation.17 | convolution fusion | flops 257417216 | bytes 3309568 | tf_op jit(solution)/shard_map/tsfcwl,wscx->fltx/dot_general | solution.py:95
  118.6 0.3 fusion.22
  119.6 1.0 copy.65
  (41 shorter events, 2.3 us)
Async XLA Ops:
  0.0 11.2 %copy-start = (bf16[8,512,256]{2,1,0:T(8,128)(2,1)S(1)}, bf16[8,512,256]{2,1,0:T(8,128)(2,1)}, u32[]{:S(2)}) copy-start(bf16[8,512,256]{2,1,0:T(8,128)(2,1)} %param.11) | copy-start | bytes 6291460
  2.3 17.1 %copy-start.5 = (bf16[128,128]{1,0:T(8,128)(2,1)S(1)}, bf16[128,128]{1,0:T(8,128)(2,1)}, u32[]{:S(2)}) copy-start(bf16[128,128]{1,0:T(8,128)(2,1)} %param.9) | copy-start | bytes 98308
  2.3 17.1 %copy-start.6 = (bf16[128,128]{1,0:T(8,128)(2,1)S(1)}, bf16[128,128]{1,0:T(8,128)(2,1)}, u32[]{:S(2)}) copy-start(bf16[128,128]{1,0:T(8,128)(2,1)} %param.8) | copy-start | bytes 98308
  2.3 17.1 %copy-start.7 = (f32[128]{0:T(128)S(1)}, f32[128]{0:T(128)}, u32[]{:S(2)}) copy-start(f32[128]{0:T(128)} %param.10) | copy-start | bytes 1540
  3.6 15.8 %all-to-all-start = ((bf16[8,16,1536]{2,0,1:T(8,128)(2,1)}), bf16[8,16,1536]{2,0,1:T(8,128)(2,1)S(1)}, u32[]{:S(2)}, u32[]{:S(2)}) async-start(bf16[8,16,1536]{2,0,1:T(8,128)(2,1)} %copy.52), calls=%async_computation | async-start | bytes 786432 | tf_op jit(solution)/shard_map/all_to_all | solution.py:72
  22.2 45.3 %copy-start.3 = (s32[512]{0:T(512)S(1)}, s32[512]{0:T(512)}, u32[]{:S(2)}) copy-start(s32[512]{0:T(512)} %param.12) | copy-start | bytes 6148
  22.2 45.5 %copy-start.4 = (s32[4]{0:T(128)S(1)}, s32[4]{0:T(128)}, u32[]{:S(2)}) copy-start(s32[4]{0:T(128)} %param.13) | copy-start | bytes 52
  34.4 69.6 %all-to-all-start.2 = ((bf16[64,2,768]{2,1,0:T(2,128)(2,1)}), bf16[64,2,768]{2,1,0:T(2,128)(2,1)S(1)}, u32[]{:S(2)}, u32[]{:S(2)}) async-start(bf16[64,2,768]{2,1,0:T(2,128)(2,1)} %reshape.202), calls=%async_computation.2 | async-start | bytes 393216 | tf_op jit(solution)/shard_map/all_to_all | solution.py:82
  105.6 8.5 %collective-permute-start = (bf16[2,8,3,2,64,8]{4,5,1,3,2,0:T(8,128)(2,1)S(1)}, bf16[2,8,3,2,64,8]{4,5,1,3,2,0:T(8,128)(2,1)}, u32[]{:S(2)}, u32[]{:S(2)}) collective-permute-start(bf16[2,8,3,2,64,8]{4,5,1,3,2,0:T(8,128)(2,1)S(1)} %copy.62), channel_id=1, source_target_pairs={{0,1},{1,2},{2,3},{3,4},{4,5},{5,6},{6,7},{7,8},{8,9},{9,10},{10,1... | collective-permute-start | bytes 294920 | tf_op jit(solution)/shard_map/ppermute | solution.py:101
  109.7 7.0 %collective-permute-start.1 = (bf16[2,8,3,2,64,8]{4,5,1,3,2,0:T(8,128)(2,1)S(1)}, bf16[2,8,3,2,64,8]{4,5,1,3,2,0:T(8,128)(2,1)S(1)}, u32[]{:S(2)}, u32[]{:S(2)}) collective-permute-start(bf16[2,8,3,2,64,8]{4,5,1,3,2,0:T(8,128)(2,1)S(1)} %copy.64), channel_id=1, source_target_pairs={{1,0},{2,1},{3,2},{4,3},{5,4},{6,5},{7,6},{8,7},{9,8},{10,9},{11,1... | collective-permute-start | bytes 294920 | tf_op jit(solution)/shard_map/ppermute | solution.py:102
  111.6 5.1 %copy-start.1 = (bf16[64,8,1,1280]{3,0,1,2:T(8,128)(2,1)S(1)}, bf16[64,8,1,1280]{3,0,1,2:T(8,128)(2,1)}, u32[]{:S(2)}) copy-start(bf16[64,8,1,1280]{3,0,1,2:T(8,128)(2,1)} %get-tuple-element.19) | copy-start | bytes 3932164
  111.6 5.1 %copy-start.2 = (bf16[64,8,1,1280]{3,0,1,2:T(8,128)(2,1)S(1)}, bf16[64,8,1,1280]{3,0,1,2:T(8,128)(2,1)}, u32[]{:S(2)}) copy-start(bf16[64,8,1,1280]{3,0,1,2:T(8,128)(2,1)} %get-tuple-element.20) | copy-start | bytes 3932164
